TPU v7x, 32 devices: a whole 2x2x4 slice. The times are simulated.
32 devices in a mesh: groups: 2 (over y), graph: 16 (over z, x, core).
Axes of the slice: x: 2, y: 2, z: 4, core: 2. Of those that a mesh axis runs over, the one named last changes fastest.
Arguments:
- tile_weight: bfloat16 [64, 8, 128, 128], P('graph'), may hold values from 0.00018310547 to 0.0018310547
- tile_cols: int32 [64, 8], P('graph'), may hold values from 0 to 63, as said below
- far_weight: bfloat16 [8192, 64], P('graph'), may hold values from 0.00018310547 to 0.0018310547
- send_rows: int32 [256, 4], P('graph'), may hold values from 0 to 511, as said below
- dest_links: int32 [1024], P('groups'), parts along dimension 0, may hold values from 0 to 8191
- demand: int32 [16384, 512], P(('groups', 'graph')), parts along dimension 0, may hold values from 0 to 3
- values_start: float32 [16384, 512], P(('groups', 'graph')), parts along dimension 0, may hold values from 0.15 to 6.6
Outputs:
- values: float32 [16384, 512], P(('groups', 'graph')), parts along dimension 0
- flows: float32 [16384], P(('groups', 'graph')), parts along dimension 0
There are 2 independent parts, one for each index of `groups`. A program takes and returns all parts, laid end to end along the dimension named above; an argument that names none is the same for every part. Nothing has to cross between parts.
Inputs may be any that keep to these rules, and one draw needn't show every extreme that they name: `tile_cols`: row tile t of device p = t // 4 has column tiles among p*4 - 1 to (p+1)*4, clipped to the range of tiles; each device's first row tile reads the tile just before its own, and its last row tile the tile just after. `send_rows`: local link numbers on the sending device.
All inputs are finite; a program needn't handle non-finite values.
Results may differ from a plain program's by a relative error of at most 0.0003.
Values may be sent and summed in bfloat16 or wider, within the bound.
No kernel may reach another device: no remote copies, remote signals or barrier semaphores. Data moves between devices by JAX's collectives and lax.ppermute only.
A program may use at most 128 MiB of HBM per device.

v0:
```python
import jax
import jax.numpy as jnp
from jax import lax
from jax.sharding import PartitionSpec as P

SWEEPS = 3


def passed_along(value, axis, steps):
    count = lax.axis_size(axis)
    leading, last = (max(0, -steps), min(count, count - steps))
    return lax.ppermute(value, axis, [(source, source + steps) for source in range(leading, last)])


def split_high_low(dense):
    high = lax.optimization_barrier(dense.astype(jnp.bfloat16))
    low = (dense - high.astype(jnp.float32)).astype(jnp.bfloat16)
    return high, low


def shards(tile_weight, tile_cols, far_weight, send_rows, dest_links, demand, values_start):
    tiles_here, nbrs, tile_size, _ = tile_weight.shape
    links_here = tiles_here * tile_size
    dest_count = demand.shape[1]
    peer_count = lax.axis_size("graph")
    slot_count = send_rows.shape[1]
    span = tiles_here + 2
    own_index = lax.axis_index("graph")
    local_cols = tile_cols - own_index * tiles_here + 1
    link_ids = own_index * links_here + jnp.arange(links_here, dtype=jnp.int32)
    dest_mask = (link_ids[:, None] == dest_links[None, :]).astype(jnp.float32)
    demand_flow = demand.astype(jnp.float32)
    tile_pick = (
        local_cols[:, :, None] == jnp.arange(span, dtype=jnp.int32)[None, None, :]
    ).astype(jnp.bfloat16)
    dense = jnp.einsum("tks,tkij->tisj", tile_pick, tile_weight, preferred_element_type=jnp.float32)
    dense = dense.reshape(links_here, span * tile_size)
    w_high, w_low = split_high_low(dense)
    wt_high = w_high.T
    wt_low = w_low.T
    send_flat = send_rows.reshape(-1)
    row_pick = (jnp.arange(links_here, dtype=jnp.int32)[:, None] == send_flat[None, :]).astype(
        jnp.bfloat16
    )
    row_pick_t = row_pick.T

    values = values_start
    for sweep_idx in range(SWEEPS):
        narrow = values.astype(jnp.bfloat16)
        head = narrow[:tile_size]
        tail = narrow[links_here - tile_size :]
        outgoing = jnp.dot(row_pick_t, narrow, preferred_element_type=jnp.float32).astype(jnp.bfloat16)
        outgoing = outgoing.reshape(peer_count, slot_count, dest_count)
        received = lax.all_to_all(outgoing, "graph", split_axis=0, concat_axis=0, tiled=True)
        from_prev = passed_along(tail, "graph", 1)
        from_next = passed_along(head, "graph", -1)
        padded = jnp.concatenate([from_prev, narrow, from_next], axis=0)
        near = jnp.dot(w_high, padded, preferred_element_type=jnp.float32) + jnp.dot(
            w_low, padded, preferred_element_type=jnp.float32
        )
        flat = received.reshape(-1, dest_count)
        far = jnp.dot(far_weight, flat, preferred_element_type=jnp.float32)
        values = near + far + dest_mask

    load = demand_flow
    rest_rows = links_here - tile_size
    for sweep_idx in range(SWEEPS):
        ratio = (load / values).astype(jnp.bfloat16)
        landed = jnp.dot(wt_high, ratio, preferred_element_type=jnp.float32) + jnp.dot(
            wt_low, ratio, preferred_element_type=jnp.float32
        )
        lower_rim = landed[:tile_size].astype(jnp.bfloat16)
        upper_rim = landed[tile_size + links_here :].astype(jnp.bfloat16)
        own_part = landed[tile_size : tile_size + links_here]
        far_part = lax.dot_general(
            far_weight, ratio, (((0,), (0,)), ((), ())), preferred_element_type=jnp.float32
        )
        far_part = far_part.astype(jnp.bfloat16).reshape(peer_count, slot_count, dest_count)
        returned = lax.all_to_all(far_part, "graph", split_axis=0, concat_axis=0, tiled=True)
        from_next = passed_along(lower_rim, "graph", -1).astype(jnp.float32)
        from_prev = passed_along(upper_rim, "graph", 1).astype(jnp.float32)
        own_part = (
            own_part
            + jnp.pad(from_prev, ((0, rest_rows), (0, 0)))
            + jnp.pad(from_next, ((rest_rows, 0), (0, 0)))
        )
        far_in = jnp.dot(row_pick, returned.reshape(-1, dest_count), preferred_element_type=jnp.float32)
        load = values * (own_part + far_in) + demand_flow
    flows = jnp.mean(load, axis=1)
    return (values, flows)


def solution(mesh):
    return jax.shard_map(
        shards,
        mesh=mesh,
        in_specs=(
            P("graph", None, None, None),
            P("graph", None),
            P("graph", None),
            P("graph", None),
            P("groups"),
            P(("groups", "graph"), None),
            P(("groups", "graph"), None),
        ),
        out_specs=(P(("groups", "graph"), None), P(("groups", "graph"))),
        check_vma=False,
    )
```

profile of v0, /device:TPU:0, one launch (start us, length us, event | category | flops | bytes accessed | tf_op | source)
XLA Modules:
  0.0 134.1 jit_solution(15139300225923333571)
XLA Ops:
  0.7 0.9 copy.19
  1.5 0.1 eq.45
  1.6 1.3 convert_element_type.83
  2.9 0.2 convolution_convert_fusion.5
  3.2 0.6 reshape.51
  3.8 7.4 %all-to-all-start = ((bf16[16,4,512]{2,1,0:T(4,128)(2,1)}), bf16[16,4,512]{2,1,0:T(4,128)(2,1)S(1)}, u32[]{:S(2)}, u32[]{:S(2)}) async-start(bf16[16,4,512]{2,1,0:T(4,128)(2,1)} %reshape.51), calls=%async_computation | async-start | bytes 131072 | tf_op jit(solution)/shard_map/all_to_all | solution.py:54
  11.2 0.7 fusion.53
  11.9 3.0 %collective-permute-start = (bf16[128,512]{1,0:T(8,128)(2,1)}, bf16[128,512]{1,0:T(8,128)(2,1)}, u32[]{:S(2)}, u32[]{:S(2)}) collective-permute-start(bf16[128,512]{1,0:T(8,128)(2,1)} %get-tuple-element.12), channel_id=1, source_target_pairs={{0,1},{1,2},{2,3},{3,4},{4,5},{5,6},{6,7},{7,8},{8,9},{9,10},{10,1... | collective-permute-start | bytes 393224 | tf_op jit(solution)/shard_map/ppermute | solution.py:12
  14.9 1.3 collective-permute-start.1
  16.2 0.7 fusion.23
  16.9 1.5 %copy.38 = f32[64,8,6,128]{3,1,2,0:T(8,128)} copy(f32[64,8,6,128]{3,2,1,0:T(8,128)S(1)} %bitcast.59) | data formatting | bytes 3145728
  18.5 1.9 %copy.33 = f32[512,768]{0,1:T(8,128)S(1)} copy(f32[512,768]{1,0:T(8,128)} %bitcast.60) | data formatting | bytes 3145728 | tf_op jit(solution)/shard_map/reshape | solution.py:37
  20.3 0.1 convert_element_type.82
  20.5 1.1 subtract_convert_fusion
  21.6 0.3 convolution_bitcast_fusion.2
  22.0 2.0 %fusion.29 = f32[512,512]{1,0:T(8,128)S(1)} fusion(bf16[512,768]{0,1:T(8,128)(2,1)} %subtract_convert_fusion, bf16[128,512]{1,0:T(8,128)(2,1)} %collective-permute-done.1, bf16[512,512]{1,0:T(8,128)(2,1)} %copy-done.3, bf16[128,512]{1,0:T(8,128)(2,1)} %collective-permute-done), kind=kOutput, calls=%fused_computation.56 | convolution fusion | flops 405012480 | bytes 2621440 | tf_op jit(solution)/shard_map/dot_general | solution.py:58
  24.0 1.6 %fusion.3 = bf16[512,512]{1,0:T(8,128)(2,1)S(1)} fusion(f32[512,512]{1,0:T(8,128)S(1)} %convolution_bitcast_fusion.2, f32[512,512]{1,0:T(8,128)S(1)} %fusion.29, bf16[512,768]{0,1:T(8,128)(2,1)S(1)} %convert_element_type.82, s32[512]{0:T(512)S(1)} %copy-done.9, s32[512]{0:T(512)S(1)} %iota_add_fusion, bf16[128,512]{1,0:T(8,128)(2,1)} %collective-permute-done.1, ...), kind=kOutput, calls=%fused_computation.17 | convolution fusion | flops 406585344 | bytes 4198400 | tf_op jit(solution)/shard_map/dot_general | solution.py:58
  25.7 0.2 convolution_convert_fusion.4
  25.9 0.6 reshape.53
  26.6 7.3 %all-to-all-start.1 = ((bf16[16,4,512]{2,1,0:T(4,128)(2,1)}), bf16[16,4,512]{2,1,0:T(4,128)(2,1)S(1)}, u32[]{:S(2)}, u32[]{:S(2)}) async-start(bf16[16,4,512]{2,1,0:T(4,128)(2,1)} %reshape.53), calls=%async_computation.1 | async-start | bytes 131072 | tf_op jit(solution)/shard_map/all_to_all | solution.py:54
  33.9 0.7 fusion.52
  34.6 2.9 %collective-permute-start.2 = (bf16[128,512]{1,0:T(8,128)(2,1)}, bf16[128,512]{1,0:T(8,128)(2,1)}, u32[]{:S(2)}, u32[]{:S(2)}) collective-permute-start(bf16[128,512]{1,0:T(8,128)(2,1)} %get-tuple-element.10), channel_id=1, source_target_pairs={{0,1},{1,2},{2,3},{3,4},{4,5},{5,6},{6,7},{7,8},{8,9},{9,10},{10,1... | collective-permute-start | bytes 393224 | tf_op jit(solution)/shard_map/ppermute | solution.py:12
  37.5 1.3 collective-permute-start.3
  38.8 2.0 %all-to-all-done.1 = bf16[16,4,512]{2,1,0:T(4,128)(2,1)S(1)} async-done(((bf16[16,4,512]{2,1,0:T(4,128)(2,1)}), bf16[16,4,512]{2,1,0:T(4,128)(2,1)S(1)}, u32[]{:S(2)}, u32[]{:S(2)}) %all-to-all-start.1) | async-done | bytes 65568 | tf_op jit(solution)/shard_map/all_to_all | solution.py:54
  40.8 0.3 convolution_bitcast_fusion.1
  41.2 0.2 collective-permute-done.3
  41.4 1.6 %fusion.28 = f32[512,512]{1,0:T(8,128)S(1)} fusion(bf16[512,768]{0,1:T(8,128)(2,1)S(1)} %copy-done.1, bf16[128,512]{1,0:T(8,128)(2,1)} %collective-permute-done.3, bf16[512,512]{1,0:T(8,128)(2,1)S(1)} %fusion.3, bf16[128,512]{1,0:T(8,128)(2,1)} %collective-permute-done.2), kind=kOutput, calls=%fused_computation.55 | convolution fusion | flops 405012480 | bytes 2621440 | tf_op jit(solution)/shard_map/dot_general | solution.py:58
  43.0 1.8 %fusion.4 = bf16[512,512]{1,0:T(8,128)(2,1)S(1)} fusion(f32[512,512]{1,0:T(8,128)S(1)} %convolution_bitcast_fusion.1, f32[512,512]{1,0:T(8,128)S(1)} %fusion.28, bf16[512,768]{0,1:T(8,128)(2,1)S(1)} %convert_element_type.82, s32[512]{0:T(512)S(1)} %copy-done.9, s32[512]{0:T(512)S(1)} %iota_add_fusion, bf16[128,512]{1,0:T(8,128)(2,1)} %collective-permute-done.3, ...), kind=kOutput, calls=%fused_computation.18 | convolution fusion | flops 406585344 | bytes 4198400 | tf_op jit(solution)/shard_map/dot_general | solution.py:58
  44.8 0.2 convolution_convert_fusion.3
  45.0 0.6 reshape.55
  45.6 8.7 %all-to-all-start.2 = ((bf16[16,4,512]{2,1,0:T(4,128)(2,1)}), bf16[16,4,512]{2,1,0:T(4,128)(2,1)S(1)}, u32[]{:S(2)}, u32[]{:S(2)}) async-start(bf16[16,4,512]{2,1,0:T(4,128)(2,1)} %reshape.55), calls=%async_computation.2 | async-start | bytes 131072 | tf_op jit(solution)/shard_map/all_to_all | solution.py:54
  54.3 0.7 fusion.51
  55.0 3.0 %collective-permute-start.4 = (bf16[128,512]{1,0:T(8,128)(2,1)}, bf16[128,512]{1,0:T(8,128)(2,1)}, u32[]{:S(2)}, u32[]{:S(2)}) collective-permute-start(bf16[128,512]{1,0:T(8,128)(2,1)} %get-tuple-element.8), channel_id=1, source_target_pairs={{0,1},{1,2},{2,3},{3,4},{4,5},{5,6},{6,7},{7,8},{8,9},{9,10},{10,1... | collective-permute-start | bytes 393224 | tf_op jit(solution)/shard_map/ppermute | solution.py:12
  58.0 1.3 collective-permute-start.5
  59.2 2.0 %all-to-all-done.2 = bf16[16,4,512]{2,1,0:T(4,128)(2,1)S(1)} async-done(((bf16[16,4,512]{2,1,0:T(4,128)(2,1)}), bf16[16,4,512]{2,1,0:T(4,128)(2,1)S(1)}, u32[]{:S(2)}, u32[]{:S(2)}) %all-to-all-start.2) | async-done | bytes 65568 | tf_op jit(solution)/shard_map/all_to_all | solution.py:54
  61.2 0.3 convolution_bitcast_fusion
  61.6 0.2 collective-permute-done.5
  61.8 1.6 %fusion.27 = f32[512,512]{1,0:T(8,128)S(1)} fusion(bf16[512,768]{0,1:T(8,128)(2,1)S(1)} %copy-done.1, bf16[128,512]{1,0:T(8,128)(2,1)} %collective-permute-done.5, bf16[512,512]{1,0:T(8,128)(2,1)S(1)} %fusion.4, bf16[128,512]{1,0:T(8,128)(2,1)} %collective-permute-done.4), kind=kOutput, calls=%fused_computation.54 | convolution fusion | flops 405012480 | bytes 2621440 | tf_op jit(solution)/shard_map/dot_general | solution.py:58
  63.5 2.7 %divide_convert_fusion = (bf16[512,512]{1,0:T(8,128)(2,1)S(1)}, f32[512,512]{1,0:T(8,128)}) fusion(s32[512,512]{1,0:T(8,128)S(1)} %copy-done.7, s32[512]{0:T(512)S(1)} %copy-done.9, s32[512]{0:T(512)S(1)} %iota_add_fusion, f32[512,512]{1,0:T(8,128)S(1)} %convolution_bitcast_fusion, f32[512,512]{1,0:T(8,128)S(1)} %fusion.27, ...), kind=kOutput, calls=%fused_computation.48 | convolution fusion | flops 407109632 | bytes 6295552 | tf_op jit(solution)/shard_map/dot_general | solution.py:58
  66.2 0.6 fusion.57
  66.7 1.8 %fusion.54 = (bf16[768,512]{1,0:T(8,128)(2,1)S(1)}, f32[768,512]{1,0:T(8,128)}) fusion(f32[768,512]{1,0:T(8,128)S(1)} %fusion.57, bf16[512,768]{0,1:T(8,128)(2,1)S(1)} %copy-done.1, bf16[512,512]{1,0:T(8,128)(2,1)S(1)} %get-tuple-element.14), kind=kOutput, calls=%fused_computation.85 | convolution fusion | flops 403439616 | bytes 5242880 | tf_op jit(solution)/shard_map/dot_general | solution.py:69
  68.5 0.7 fusion.50
  69.2 5.3 %collective-permute-start.6 = (bf16[128,512]{1,0:T(8,128)(2,1)}, bf16[128,512]{1,0:T(8,128)(2,1)S(1)}, u32[]{:S(2)}, u32[]{:S(2)}) collective-permute-start(bf16[128,512]{1,0:T(8,128)(2,1)} %get-tuple-element.6), channel_id=1, source_target_pairs={{0,1},{1,2},{2,3},{3,4},{4,5},{5,6},{6,7},{7,8},{8,9},{9,10},{10,1... | collective-permute-start | bytes 393224 | tf_op jit(solution)/shard_map/ppermute | solution.py:12
  74.6 1.3 collective-permute-start.7
  75.9 0.2 fusion.5
  76.1 13.9 %all_to_all.30 = bf16[16,4,512]{2,1,0:T(4,128)(2,1)S(1)} all-to-all(bf16[16,4,512]{2,1,0:T(4,128)(2,1)S(1)} %reshape.57), channel_id=1, replica_groups=mesh['groups'=2,'graph'=16] {'graph'}, dimensions={0} | all-to-all | bytes 131072 | tf_op jit(solution)/shard_map/all_to_all | solution.py:79
  90.1 2.3 %fusion.25 = bf16[512,512]{1,0:T(8,128)(2,1)S(1)} fusion(f32[512,512]{1,0:T(8,128)} %get-tuple-element.15, s32[512,512]{1,0:T(8,128)} %param.12, f32[768,512]{1,0:T(8,128)} %get-tuple-element.17, bf16[128,512]{1,0:T(8,128)(2,1)S(1)} %collective-permute-done.7, bf16[128,512]{1,0:T(8,128)(2,1)S(1)} %collective-permute-done.6, ...), kind=kOutput, calls=%fused_computation.49 | convolution fusion | flops 36208640 | bytes 3997952 | tf_op jit(solution)/shard_map/dot_general | solution.py:87
  92.4 0.6 fusion.58
  92.9 1.8 %fusion.55 = (bf16[768,512]{1,0:T(8,128)(2,1)S(1)}, f32[768,512]{1,0:T(8,128)}) fusion(f32[768,512]{1,0:T(8,128)S(1)} %fusion.58, bf16[512,768]{0,1:T(8,128)(2,1)S(1)} %copy-done.1, bf16[512,512]{1,0:T(8,128)(2,1)S(1)} %fusion.25), kind=kOutput, calls=%fused_computation.86 | convolution fusion | flops 403439616 | bytes 5242880 | tf_op jit(solution)/shard_map/dot_general | solution.py:69
  94.7 0.7 fusion.49
  95.4 1.4 %collective-permute-start.8 = (bf16[128,512]{1,0:T(8,128)(2,1)}, bf16[128,512]{1,0:T(8,128)(2,1)S(1)}, u32[]{:S(2)}, u32[]{:S(2)}) collective-permute-start(bf16[128,512]{1,0:T(8,128)(2,1)} %get-tuple-element.4), channel_id=1, source_target_pairs={{0,1},{1,2},{2,3},{3,4},{4,5},{5,6},{6,7},{7,8},{8,9},{9,10},{10,1... | collective-permute-start | bytes 393224 | tf_op jit(solution)/shard_map/ppermute | solution.py:12
  96.9 1.3 collective-permute-start.9
  98.2 0.2 fusion.6
  98.4 12.3 %all_to_all.31 = bf16[16,4,512]{2,1,0:T(4,128)(2,1)S(1)} all-to-all(bf16[16,4,512]{2,1,0:T(4,128)(2,1)S(1)} %reshape.59), channel_id=1, replica_groups=mesh['groups'=2,'graph'=16] {'graph'}, dimensions={0} | all-to-all | bytes 131072 | tf_op jit(solution)/shard_map/all_to_all | solution.py:79
  110.8 2.3 %fusion.26 = bf16[512,512]{1,0:T(8,128)(2,1)S(1)} fusion(f32[512,512]{1,0:T(8,128)} %get-tuple-element.15, s32[512,512]{1,0:T(8,128)} %param.12, f32[768,512]{1,0:T(8,128)} %get-tuple-element.19, bf16[128,512]{1,0:T(8,128)(2,1)S(1)} %collective-permute-done.9, bf16[128,512]{1,0:T(8,128)(2,1)S(1)} %collective-permute-done.8, ...), kind=kOutput, calls=%fused_computation.50 | convolution fusion | flops 36208640 | bytes 3997952 | tf_op jit(solution)/shard_map/dot_general | solution.py:87
  113.1 0.6 fusion.59
  113.6 1.7 %fusion.56 = (bf16[768,512]{1,0:T(8,128)(2,1)S(1)}, f32[768,512]{1,0:T(8,128)}) fusion(f32[768,512]{1,0:T(8,128)S(1)} %fusion.59, bf16[512,768]{0,1:T(8,128)(2,1)S(1)} %copy-done.1, bf16[512,512]{1,0:T(8,128)(2,1)S(1)} %fusion.26), kind=kOutput, calls=%fused_computation.87 | convolution fusion | flops 403439616 | bytes 5242880 | tf_op jit(solution)/shard_map/dot_general | solution.py:69
  115.4 0.7 fusion.48
  116.1 1.5 %collective-permute-start.10 = (bf16[128,512]{1,0:T(8,128)(2,1)}, bf16[128,512]{1,0:T(8,128)(2,1)S(1)}, u32[]{:S(2)}, u32[]{:S(2)}) collective-permute-start(bf16[128,512]{1,0:T(8,128)(2,1)} %get-tuple-element.2), channel_id=1, source_target_pairs={{0,1},{1,2},{2,3},{3,4},{4,5},{5,6},{6,7},{7,8},{8,9},{9,10},{10,1... | collective-permute-start | bytes 393224 | tf_op jit(solution)/shard_map/ppermute | solution.py:12
  117.6 1.3 collective-permute-start.11
  118.9 0.2 fusion.7
  119.1 12.3 %all_to_all.32 = bf16[16,4,512]{2,1,0:T(4,128)(2,1)S(1)} all-to-all(bf16[16,4,512]{2,1,0:T(4,128)(2,1)S(1)} %reshape.61), channel_id=1, replica_groups=mesh['groups'=2,'graph'=16] {'graph'}, dimensions={0} | all-to-all | bytes 131072 | tf_op jit(solution)/shard_map/all_to_all | solution.py:79
  131.5 2.0 %fusion.12 = f32[512]{0:T(512)S(1)} fusion(f32[512,512]{1,0:T(8,128)} %get-tuple-element.15, f32[768,512]{1,0:T(8,128)S(1)} %copy-done.2, s32[512,512]{1,0:T(8,128)} %param.12, bf16[128,512]{1,0:T(8,128)(2,1)S(1)} %collective-permute-done.11, bf16[128,512]{1,0:T(8,128)(2,1)S(1)} %collective-permute-done.10, bf16[64,512]{1,0:T(8,128)(2,1)S(1)} %reshape.62, ...), kind=kOutput, calls=%fused_computation.33 | convolution fusion | flops 35945984 | bytes 3475712 | tf_op jit(solution)/shard_map/dot_general | solution.py:87
  133.5 0.6 broadcast_multiply_fusion
  (42 shorter events, 0.3 us)
Async XLA Ops:
  0.6 15.6 %copy-start = (bf16[4,8,128,128]{3,2,1,0:T(8,128)(2,1)S(1)}, bf16[4,8,128,128]{3,2,1,0:T(8,128)(2,1)}, u32[]{:S(2)}) copy-start(bf16[4,8,128,128]{3,2,1,0:T(8,128)(2,1)} %param.7) | copy-start | bytes 3145732
  0.6 15.5 %copy-start.8 = (s32[4,8]{1,0:T(4,128)S(1)}, s32[4,8]{1,0:T(4,128)}, u32[]{:S(2)}) copy-start(s32[4,8]{1,0:T(4,128)} %param.8) | copy-start | bytes 388
  2.9 15.6 %copy-start.3 = (bf16[512,512]{1,0:T(8,128)(2,1)}, bf16[512,512]{1,0:T(8,128)(2,1)S(1)}, u32[]{:S(2)}) copy-start(bf16[512,512]{1,0:T(8,128)(2,1)S(1)} %convert_element_type.83) | copy-start | bytes 1572868
  3.8 17.8 %all-to-all-start = ((bf16[16,4,512]{2,1,0:T(4,128)(2,1)}), bf16[16,4,512]{2,1,0:T(4,128)(2,1)S(1)}, u32[]{:S(2)}, u32[]{:S(2)}) async-start(bf16[16,4,512]{2,1,0:T(4,128)(2,1)} %reshape.51), calls=%async_computation | async-start | bytes 131072 | tf_op jit(solution)/shard_map/all_to_all | solution.py:54
  11.9 10.1 %collective-permute-start = (bf16[128,512]{1,0:T(8,128)(2,1)}, bf16[128,512]{1,0:T(8,128)(2,1)}, u32[]{:S(2)}, u32[]{:S(2)}) collective-permute-start(bf16[128,512]{1,0:T(8,128)(2,1)} %get-tuple-element.12), channel_id=1, source_target_pairs={{0,1},{1,2},{2,3},{3,4},{4,5},{5,6},{6,7},{7,8},{8,9},{9,10},{10,1... | collective-permute-start | bytes 393224 | tf_op jit(solution)/shard_map/ppermute | solution.py:12
  14.9 7.1 %collective-permute-start.1 = (bf16[128,512]{1,0:T(8,128)(2,1)}, bf16[128,512]{1,0:T(8,128)(2,1)}, u32[]{:S(2)}, u32[]{:S(2)}) collective-permute-start(bf16[128,512]{1,0:T(8,128)(2,1)} %get-tuple-element.13), channel_id=1, source_target_pairs={{1,0},{2,1},{3,2},{4,3},{5,4},{6,5},{7,6},{8,7},{9,8},{10,9},{11,1... | collective-permute-start | bytes 393224 | tf_op jit(solution)/shard_map/ppermute | solution.py:12
  20.4 1.2 copy-start.5
  22.0 2.0 %copy-start.4 = (bf16[512,512]{1,0:T(8,128)(2,1)S(1)}, bf16[512,512]{1,0:T(8,128)(2,1)}, u32[]{:S(2)}) copy-start(bf16[512,512]{1,0:T(8,128)(2,1)} %copy-done.3) | copy-start | bytes 1572868
  22.0 2.0 %copy-start.9 = (s32[512]{0:T(512)S(1)}, s32[512]{0:T(512)}, u32[]{:S(2)}) copy-start(s32[512]{0:T(512)} %param.11) | copy-start | bytes 6148
  25.7 15.7 %copy-start.6 = (bf16[512,512]{1,0:T(8,128)(2,1)}, bf16[512,512]{1,0:T(8,128)(2,1)S(1)}, u32[]{:S(2)}) copy-start(bf16[512,512]{1,0:T(8,128)(2,1)S(1)} %fusion.3) | copy-start | bytes 1572868
  25.7 15.7 %copy-start.1 = (bf16[512,768]{0,1:T(8,128)(2,1)S(1)}, bf16[512,768]{0,1:T(8,128)(2,1)}, u32[]{:S(2)}) copy-start(bf16[512,768]{0,1:T(8,128)(2,1)} %subtract_convert_fusion) | copy-start | bytes 2359300
  26.6 14.2 %all-to-all-start.1 = ((bf16[16,4,512]{2,1,0:T(4,128)(2,1)}), bf16[16,4,512]{2,1,0:T(4,128)(2,1)S(1)}, u32[]{:S(2)}, u32[]{:S(2)}) async-start(bf16[16,4,512]{2,1,0:T(4,128)(2,1)} %reshape.53), calls=%async_computation.1 | async-start | bytes 131072 | tf_op jit(solution)/shard_map/all_to_all | solution.py:54
  34.6 6.6 %collective-permute-start.2 = (bf16[128,512]{1,0:T(8,128)(2,1)}, bf16[128,512]{1,0:T(8,128)(2,1)}, u32[]{:S(2)}, u32[]{:S(2)}) collective-permute-start(bf16[128,512]{1,0:T(8,128)(2,1)} %get-tuple-element.10), channel_id=1, source_target_pairs={{0,1},{1,2},{2,3},{3,4},{4,5},{5,6},{6,7},{7,8},{8,9},{9,10},{10,1... | collective-permute-start | bytes 393224 | tf_op jit(solution)/shard_map/ppermute | solution.py:12
  37.5 3.9 %collective-permute-start.3 = (bf16[128,512]{1,0:T(8,128)(2,1)S(1)}, bf16[128,512]{1,0:T(8,128)(2,1)}, u32[]{:S(2)}, u32[]{:S(2)}) collective-permute-start(bf16[128,512]{1,0:T(8,128)(2,1)S(1)} %get-tuple-element.11), channel_id=1, source_target_pairs={{1,0},{2,1},{3,2},{4,3},{5,4},{6,5},{7,6},{8,7},{9,8},{10,9},{11,1... | collective-permute-start | bytes 393224 | tf_op jit(solution)/shard_map/ppermute | solution.py:12
  45.6 15.6 %all-to-all-start.2 = ((bf16[16,4,512]{2,1,0:T(4,128)(2,1)}), bf16[16,4,512]{2,1,0:T(4,128)(2,1)S(1)}, u32[]{:S(2)}, u32[]{:S(2)}) async-start(bf16[16,4,512]{2,1,0:T(4,128)(2,1)} %reshape.55), calls=%async_computation.2 | async-start | bytes 131072 | tf_op jit(solution)/shard_map/all_to_all | solution.py:54
  55.0 6.6 %collective-permute-start.4 = (bf16[128,512]{1,0:T(8,128)(2,1)}, bf16[128,512]{1,0:T(8,128)(2,1)}, u32[]{:S(2)}, u32[]{:S(2)}) collective-permute-start(bf16[128,512]{1,0:T(8,128)(2,1)} %get-tuple-element.8), channel_id=1, source_target_pairs={{0,1},{1,2},{2,3},{3,4},{4,5},{5,6},{6,7},{7,8},{8,9},{9,10},{10,1... | collective-permute-start | bytes 393224 | tf_op jit(solution)/shard_map/ppermute | solution.py:12
  58.0 3.9 %collective-permute-start.5 = (bf16[128,512]{1,0:T(8,128)(2,1)S(1)}, bf16[128,512]{1,0:T(8,128)(2,1)}, u32[]{:S(2)}, u32[]{:S(2)}) collective-permute-start(bf16[128,512]{1,0:T(8,128)(2,1)S(1)} %get-tuple-element.9), channel_id=1, source_target_pairs={{1,0},{2,1},{3,2},{4,3},{5,4},{6,5},{7,6},{8,7},{9,8},{10,9},{11,1... | collective-permute-start | bytes 393224 | tf_op jit(solution)/shard_map/ppermute | solution.py:12
  61.6 1.9 %copy-start.7 = (s32[512,512]{1,0:T(8,128)S(1)}, s32[512,512]{1,0:T(8,128)}, u32[]{:S(2)}) copy-start(s32[512,512]{1,0:T(8,128)} %param.12) | copy-start | bytes 3145732
  69.2 20.8 %collective-permute-start.6 = (bf16[128,512]{1,0:T(8,128)(2,1)}, bf16[128,512]{1,0:T(8,128)(2,1)S(1)}, u32[]{:S(2)}, u32[]{:S(2)}) collective-permute-start(bf16[128,512]{1,0:T(8,128)(2,1)} %get-tuple-element.6), channel_id=1, source_target_pairs={{0,1},{1,2},{2,3},{3,4},{4,5},{5,6},{6,7},{7,8},{8,9},{9,10},{10,1... | collective-permute-start | bytes 393224 | tf_op jit(solution)/shard_map/ppermute | solution.py:12
  74.6 15.5 %collective-permute-start.7 = (bf16[128,512]{1,0:T(8,128)(2,1)}, bf16[128,512]{1,0:T(8,128)(2,1)S(1)}, u32[]{:S(2)}, u32[]{:S(2)}) collective-permute-start(bf16[128,512]{1,0:T(8,128)(2,1)} %get-tuple-element.7), channel_id=1, source_target_pairs={{1,0},{2,1},{3,2},{4,3},{5,4},{6,5},{7,6},{8,7},{9,8},{10,9},{11,1... | collective-permute-start | bytes 393224 | tf_op jit(solution)/shard_map/ppermute | solution.py:12
  95.4 15.4 %collective-permute-start.8 = (bf16[128,512]{1,0:T(8,128)(2,1)}, bf16[128,512]{1,0:T(8,128)(2,1)S(1)}, u32[]{:S(2)}, u32[]{:S(2)}) collective-permute-start(bf16[128,512]{1,0:T(8,128)(2,1)} %get-tuple-element.4), channel_id=1, source_target_pairs={{0,1},{1,2},{2,3},{3,4},{4,5},{5,6},{6,7},{7,8},{8,9},{9,10},{10,1... | collective-permute-start | bytes 393224 | tf_op jit(solution)/shard_map/ppermute | solution.py:12
  96.9 13.9 %collective-permute-start.9 = (bf16[128,512]{1,0:T(8,128)(2,1)}, bf16[128,512]{1,0:T(8,128)(2,1)S(1)}, u32[]{:S(2)}, u32[]{:S(2)}) collective-permute-start(bf16[128,512]{1,0:T(8,128)(2,1)} %get-tuple-element.5), channel_id=1, source_target_pairs={{1,0},{2,1},{3,2},{4,3},{5,4},{6,5},{7,6},{8,7},{9,8},{10,9},{11,1... | collective-permute-start | bytes 393224 | tf_op jit(solution)/shard_map/ppermute | solution.py:12
  115.4 16.1 %copy-start.2 = (f32[768,512]{1,0:T(8,128)S(1)}, f32[768,512]{1,0:T(8,128)}, u32[]{:S(2)}) copy-start(f32[768,512]{1,0:T(8,128)} %get-tuple-element.21) | copy-start | bytes 4718596
  116.1 15.4 %collective-permute-start.10 = (bf16[128,512]{1,0:T(8,128)(2,1)}, bf16[128,512]{1,0:T(8,128)(2,1)S(1)}, u32[]{:S(2)}, u32[]{:S(2)}) collective-permute-start(bf16[128,512]{1,0:T(8,128)(2,1)} %get-tuple-element.2), channel_id=1, source_target_pairs={{0,1},{1,2},{2,3},{3,4},{4,5},{5,6},{6,7},{7,8},{8,9},{9,10},{10,1... | collective-permute-start | bytes 393224 | tf_op jit(solution)/shard_map/ppermute | solution.py:12
  117.6 13.9 %collective-permute-start.11 = (bf16[128,512]{1,0:T(8,128)(2,1)}, bf16[128,512]{1,0:T(8,128)(2,1)S(1)}, u32[]{:S(2)}, u32[]{:S(2)}) collective-permute-start(bf16[128,512]{1,0:T(8,128)(2,1)} %get-tuple-element.3), channel_id=1, source_target_pairs={{1,0},{2,1},{3,2},{4,3},{5,4},{6,5},{7,6},{8,7},{9,8},{10,9},{11,1... | collective-permute-start | bytes 393224 | tf_op jit(solution)/shard_map/ppermute | solution.py:12
where the time goes:
time: 135 us; the launch traced here: 134 us
  starting transfers between devices  48.2 us (36%)
  blocking collectives  38.6 us (29%)
  matrix products  27.8 us (21%)
  local copies, waits for them, and re-layouts  10.8 us (8%)
  waiting for transfers between devices  4.43 us (3%)
  other arithmetic  3.13 us (2%)
    all_to_all x3, blocking collectives, shards(): lax.all_to_all(far_part, 'graph', split_axis=0, concat_axis=0, tiled=True)  38.6 us
    ppermute x12, starting transfers between devices, passed_along(): lax.ppermute(value, axis, [(source, source + steps) for source in range(l...  24.8 us
    all_to_all x3, starting transfers between devices, shards(): lax.all_to_all(outgoing, 'graph', split_axis=0, concat_axis=0, tiled=True)  23.4 us
    dot_general x3, matrix products, shards(): jnp.dot(row_pick, returned.reshape(-1, dest_count), preferred_element_typ...  6.5 us
    dot_general x3, matrix products, shards(): jnp.dot(w_high, padded, preferred_element_type=jnp.float32)  6.11 us
    dot_general x3, matrix products, shards(): jnp.dot(wt_low, ratio, preferred_element_type=jnp.float32)  5.25 us
    dot_general x3, matrix products, shards(): jnp.dot(w_low, padded, preferred_element_type=jnp.float32)  5.19 us
    all_to_all x3, waiting for transfers between devices, shards(): lax.all_to_all(outgoing, 'graph', split_axis=0, concat_axis=0, tiled=True)  3.97 us
  transfers between devices with their start and end apart: 15, of which 4 were waited for; matrix products, arithmetic and copies ran while one was open for 7% of the time, Pallas kernels for 0%

commit v1 on v0

--- a/solution.py
+++ b/solution.py
@@ -8,8 +8,7 @@
 
 def passed_along(value, axis, steps):
     count = lax.axis_size(axis)
-    leading, last = (max(0, -steps), min(count, count - steps))
-    return lax.ppermute(value, axis, [(source, source + steps) for source in range(leading, last)])
+    return lax.ppermute(value, axis, [(source, (source + steps) % count) for source in range(count)])
 
 
 def split_high_low(dense):

time: 135 us -> 120 us (0.89)
  blocking collectives: 38.6 us -> 28.4 us
  starting transfers between devices: 48.2 us -> 42.8 us
  waiting for transfers between devices: 4.43 us -> 5.82 us
    all_to_all x3, blocking collectives: 38.6 us -> 28.4 us  [shards(): lax.all_to_all(far_part, 'graph', split_axis=0, concat_axis=0, tiled=True)]
    all_to_all x3, starting transfers between devices: 23.4 us -> 16.2 us  [shards(): lax.all_to_all(outgoing, 'graph', split_axis=0, concat_axis=0, tiled=True)]
    ppermute x12, starting transfers between devices: 24.8 us -> 26.7 us  [passed_along(): lax.ppermute(value, axis, [(source, (source + steps) % count) for source...]
  transfers between devices with their start and end apart: 15 -> 15, of which waited for: 4 -> 4; matrix products, arithmetic and copies ran while one was open for 7% -> 8% of each run, Pallas kernels for 0% -> 0%
where the time goes in v1:
time: 120 us
  starting transfers between devices  42.8 us (36%)
  blocking collectives  28.4 us (24%)
  matrix products  27.7 us (23%)
  local copies, waits for them, and re-layouts  10.8 us (9%)
  waiting for transfers between devices  5.82 us (5%)
  other arithmetic  3.13 us (3%)
    all_to_all x3, blocking collectives, shards(): lax.all_to_all(far_part, 'graph', split_axis=0, concat_axis=0, tiled=True)  28.4 us
    ppermute x12, starting transfers between devices, passed_along(): lax.ppermute(value, axis, [(source, (source + steps) % count) for source...  26.7 us
    all_to_all x3, starting transfers between devices, shards(): lax.all_to_all(outgoing, 'graph', split_axis=0, concat_axis=0, tiled=True)  16.2 us
    dot_general x3, matrix products, shards(): jnp.dot(row_pick, returned.reshape(-1, dest_count), preferred_element_typ...  6.5 us
    dot_general x3, matrix products, shards(): jnp.dot(w_high, padded, preferred_element_type=jnp.float32)  6.11 us
    dot_general x3, matrix products, shards(): jnp.dot(wt_low, ratio, preferred_element_type=jnp.float32)  5.24 us
    dot_general x3, matrix products, shards(): jnp.dot(w_low, padded, preferred_element_type=jnp.float32)  5.11 us
    all_to_all x3, waiting for transfers between devices, shards(): lax.all_to_all(outgoing, 'graph', split_axis=0, concat_axis=0, tiled=True)  4.14 us
  transfers between devices with their start and end apart: 15, of which 4 were waited for; matrix products, arithmetic and copies ran while one was open for 8% of the time, Pallas kernels for 0%

profile of v1, /device:TPU:0, one launch (start us, length us, event | category | flops | bytes accessed | tf_op | source)
XLA Modules:
  0.0 119.7 jit_solution(4716756344511778437)
XLA Ops:
  0.6 0.0 copy-start
  0.7 0.9 copy.19
  1.5 0.1 eq.45
  1.6 1.3 %convert_element_type.83 = bf16[512,512]{1,0:T(8,128)(2,1)S(1)} convert(f32[512,512]{1,0:T(8,128)} %param.13) | non-fusion elementwise | flops 262144 | bytes 1572864 | tf_op jit(solution)/shard_map/convert_element_type | solution.py:48
  2.9 0.2 convolution_convert_fusion.5
  3.2 0.6 reshape.51
  3.8 7.4 %all-to-all-start = ((bf16[16,4,512]{2,1,0:T(4,128)(2,1)}), bf16[16,4,512]{2,1,0:T(4,128)(2,1)S(1)}, u32[]{:S(2)}, u32[]{:S(2)}) async-start(bf16[16,4,512]{2,1,0:T(4,128)(2,1)} %reshape.51), calls=%async_computation | async-start | bytes 131072 | tf_op jit(solution)/shard_map/all_to_all | solution.py:53
  11.2 0.7 fusion.53
  11.9 0.4 collective-permute-start
  12.3 4.0 %collective-permute-start.1 = (bf16[128,512]{1,0:T(8,128)(2,1)}, bf16[128,512]{1,0:T(8,128)(2,1)}, u32[]{:S(2)}, u32[]{:S(2)}) collective-permute-start(bf16[128,512]{1,0:T(8,128)(2,1)} %get-tuple-element.13), channel_id=1, source_target_pairs={{0,15},{1,0},{2,1},{3,2},{4,3},{5,4},{6,5},{7,6},{8,7},{9,8},{10,9... | collective-permute-start | bytes 393224 | tf_op jit(solution)/shard_map/ppermute | solution.py:11
  16.4 0.7 fusion.23
  17.1 1.5 %copy.38 = f32[64,8,6,128]{3,1,2,0:T(8,128)} copy(f32[64,8,6,128]{3,2,1,0:T(8,128)S(1)} %bitcast.59) | data formatting | bytes 3145728
  18.6 1.9 %copy.33 = f32[512,768]{0,1:T(8,128)S(1)} copy(f32[512,768]{1,0:T(8,128)} %bitcast.60) | data formatting | bytes 3145728 | tf_op jit(solution)/shard_map/reshape | solution.py:36
  20.5 0.1 convert_element_type.82
  20.6 0.0 copy-start.5
  20.6 1.1 subtract_convert_fusion
  21.8 0.3 convolution_bitcast_fusion.2
  22.2 2.0 %fusion.29 = f32[512,512]{1,0:T(8,128)S(1)} fusion(bf16[512,768]{0,1:T(8,128)(2,1)} %subtract_convert_fusion, bf16[128,512]{1,0:T(8,128)(2,1)} %collective-permute-done.1, bf16[512,512]{1,0:T(8,128)(2,1)} %copy-done.3, bf16[128,512]{1,0:T(8,128)(2,1)} %collective-permute-done), kind=kOutput, calls=%fused_computation.56 | convolution fusion | flops 405012480 | bytes 2621440 | tf_op jit(solution)/shard_map/dot_general | solution.py:57
  24.2 1.6 %fusion.3 = bf16[512,512]{1,0:T(8,128)(2,1)S(1)} fusion(f32[512,512]{1,0:T(8,128)S(1)} %convolution_bitcast_fusion.2, f32[512,512]{1,0:T(8,128)S(1)} %fusion.29, bf16[512,768]{0,1:T(8,128)(2,1)S(1)} %convert_element_type.82, s32[512]{0:T(512)S(1)} %copy-done.9, s32[512]{0:T(512)S(1)} %iota_add_fusion, bf16[128,512]{1,0:T(8,128)(2,1)} %collective-permute-done.1, ...), kind=kOutput, calls=%fused_computation.17 | convolution fusion | flops 406585344 | bytes 4198400 | tf_op jit(solution)/shard_map/dot_general | solution.py:57
  25.8 0.2 convolution_convert_fusion.4
  26.1 0.6 reshape.53
  26.7 3.5 %all-to-all-start.1 = ((bf16[16,4,512]{2,1,0:T(4,128)(2,1)}), bf16[16,4,512]{2,1,0:T(4,128)(2,1)S(1)}, u32[]{:S(2)}, u32[]{:S(2)}) async-start(bf16[16,4,512]{2,1,0:T(4,128)(2,1)} %reshape.53), calls=%async_computation.1 | async-start | bytes 131072 | tf_op jit(solution)/shard_map/all_to_all | solution.py:53
  30.2 0.7 fusion.52
  30.9 0.3 collective-permute-start.2
  31.2 4.2 %collective-permute-start.3 = (bf16[128,512]{1,0:T(8,128)(2,1)S(1)}, bf16[128,512]{1,0:T(8,128)(2,1)}, u32[]{:S(2)}, u32[]{:S(2)}) collective-permute-start(bf16[128,512]{1,0:T(8,128)(2,1)S(1)} %get-tuple-element.11), channel_id=1, source_target_pairs={{0,15},{1,0},{2,1},{3,2},{4,3},{5,4},{6,5},{7,6},{8,7},{9,8},{10,9... | collective-permute-start | bytes 393224 | tf_op jit(solution)/shard_map/ppermute | solution.py:11
  35.4 2.0 %all-to-all-done.1 = bf16[16,4,512]{2,1,0:T(4,128)(2,1)S(1)} async-done(((bf16[16,4,512]{2,1,0:T(4,128)(2,1)}), bf16[16,4,512]{2,1,0:T(4,128)(2,1)S(1)}, u32[]{:S(2)}, u32[]{:S(2)}) %all-to-all-start.1) | async-done | bytes 65568 | tf_op jit(solution)/shard_map/all_to_all | solution.py:53
  37.4 0.3 convolution_bitcast_fusion.1
  37.8 0.9 collective-permute-done.2
  38.6 1.6 %fusion.28 = f32[512,512]{1,0:T(8,128)S(1)} fusion(bf16[512,768]{0,1:T(8,128)(2,1)S(1)} %copy-done.1, bf16[128,512]{1,0:T(8,128)(2,1)} %collective-permute-done.3, bf16[512,512]{1,0:T(8,128)(2,1)S(1)} %fusion.3, bf16[128,512]{1,0:T(8,128)(2,1)} %collective-permute-done.2), kind=kOutput, calls=%fused_computation.55 | convolution fusion | flops 405012480 | bytes 2621440 | tf_op jit(solution)/shard_map/dot_general | solution.py:57
  40.2 1.8 %fusion.4 = bf16[512,512]{1,0:T(8,128)(2,1)S(1)} fusion(f32[512,512]{1,0:T(8,128)S(1)} %convolution_bitcast_fusion.1, f32[512,512]{1,0:T(8,128)S(1)} %fusion.28, bf16[512,768]{0,1:T(8,128)(2,1)S(1)} %convert_element_type.82, s32[512]{0:T(512)S(1)} %copy-done.9, s32[512]{0:T(512)S(1)} %iota_add_fusion, bf16[128,512]{1,0:T(8,128)(2,1)} %collective-permute-done.3, ...), kind=kOutput, calls=%fused_computation.18 | convolution fusion | flops 406585344 | bytes 4198400 | tf_op jit(solution)/shard_map/dot_general | solution.py:57
  42.0 0.2 convolution_convert_fusion.3
  42.2 0.6 reshape.55
  42.9 5.3 %all-to-all-start.2 = ((bf16[16,4,512]{2,1,0:T(4,128)(2,1)}), bf16[16,4,512]{2,1,0:T(4,128)(2,1)S(1)}, u32[]{:S(2)}, u32[]{:S(2)}) async-start(bf16[16,4,512]{2,1,0:T(4,128)(2,1)} %reshape.55), calls=%async_computation.2 | async-start | bytes 131072 | tf_op jit(solution)/shard_map/all_to_all | solution.py:53
  48.2 0.7 fusion.51
  48.9 0.4 collective-permute-start.4
  49.3 4.0 %collective-permute-start.5 = (bf16[128,512]{1,0:T(8,128)(2,1)S(1)}, bf16[128,512]{1,0:T(8,128)(2,1)}, u32[]{:S(2)}, u32[]{:S(2)}) collective-permute-start(bf16[128,512]{1,0:T(8,128)(2,1)S(1)} %get-tuple-element.9), channel_id=1, source_target_pairs={{0,15},{1,0},{2,1},{3,2},{4,3},{5,4},{6,5},{7,6},{8,7},{9,8},{10,9... | collective-permute-start | bytes 393224 | tf_op jit(solution)/shard_map/ppermute | solution.py:11
  53.3 2.1 %all-to-all-done.2 = bf16[16,4,512]{2,1,0:T(4,128)(2,1)S(1)} async-done(((bf16[16,4,512]{2,1,0:T(4,128)(2,1)}), bf16[16,4,512]{2,1,0:T(4,128)(2,1)S(1)}, u32[]{:S(2)}, u32[]{:S(2)}) %all-to-all-start.2) | async-done | bytes 65568 | tf_op jit(solution)/shard_map/all_to_all | solution.py:53
  55.4 0.3 convolution_bitcast_fusion
  55.8 0.8 collective-permute-done.4
  56.6 1.6 %fusion.27 = f32[512,512]{1,0:T(8,128)S(1)} fusion(bf16[512,768]{0,1:T(8,128)(2,1)S(1)} %copy-done.1, bf16[128,512]{1,0:T(8,128)(2,1)} %collective-permute-done.5, bf16[512,512]{1,0:T(8,128)(2,1)S(1)} %fusion.4, bf16[128,512]{1,0:T(8,128)(2,1)} %collective-permute-done.4), kind=kOutput, calls=%fused_computation.54 | convolution fusion | flops 405012480 | bytes 2621440 | tf_op jit(solution)/shard_map/dot_general | solution.py:57
  58.2 2.7 %divide_convert_fusion = (bf16[512,512]{1,0:T(8,128)(2,1)S(1)}, f32[512,512]{1,0:T(8,128)}) fusion(s32[512,512]{1,0:T(8,128)S(1)} %copy-done.7, s32[512]{0:T(512)S(1)} %copy-done.9, s32[512]{0:T(512)S(1)} %iota_add_fusion, f32[512,512]{1,0:T(8,128)S(1)} %convolution_bitcast_fusion, f32[512,512]{1,0:T(8,128)S(1)} %fusion.27, ...), kind=kOutput, calls=%fused_computation.48 | convolution fusion | flops 407109632 | bytes 6295552 | tf_op jit(solution)/shard_map/dot_general | solution.py:57
  60.9 0.6 fusion.57
  61.4 1.8 %fusion.54 = (bf16[768,512]{1,0:T(8,128)(2,1)S(1)}, f32[768,512]{1,0:T(8,128)}) fusion(f32[768,512]{1,0:T(8,128)S(1)} %fusion.57, bf16[512,768]{0,1:T(8,128)(2,1)S(1)} %copy-done.1, bf16[512,512]{1,0:T(8,128)(2,1)S(1)} %get-tuple-element.14), kind=kOutput, calls=%fused_computation.85 | convolution fusion | flops 403439616 | bytes 5242880 | tf_op jit(solution)/shard_map/dot_general | solution.py:68
  63.2 0.7 fusion.50
  63.9 0.4 collective-permute-start.6
  64.3 4.1 %collective-permute-start.7 = (bf16[128,512]{1,0:T(8,128)(2,1)}, bf16[128,512]{1,0:T(8,128)(2,1)S(1)}, u32[]{:S(2)}, u32[]{:S(2)}) collective-permute-start(bf16[128,512]{1,0:T(8,128)(2,1)} %get-tuple-element.7), channel_id=1, source_target_pairs={{0,15},{1,0},{2,1},{3,2},{4,3},{5,4},{6,5},{7,6},{8,7},{9,8},{10,9... | collective-permute-start | bytes 393224 | tf_op jit(solution)/shard_map/ppermute | solution.py:11
  68.4 0.2 fusion.5
  68.6 9.5 %all_to_all.30 = bf16[16,4,512]{2,1,0:T(4,128)(2,1)S(1)} all-to-all(bf16[16,4,512]{2,1,0:T(4,128)(2,1)S(1)} %reshape.57), channel_id=1, replica_groups=mesh['groups'=2,'graph'=16] {'graph'}, dimensions={0} | all-to-all | bytes 131072 | tf_op jit(solution)/shard_map/all_to_all | solution.py:78
  78.1 2.3 %fusion.25 = bf16[512,512]{1,0:T(8,128)(2,1)S(1)} fusion(f32[512,512]{1,0:T(8,128)} %get-tuple-element.15, s32[512,512]{1,0:T(8,128)} %param.12, f32[768,512]{1,0:T(8,128)} %get-tuple-element.17, bf16[128,512]{1,0:T(8,128)(2,1)S(1)} %collective-permute-done.7, bf16[128,512]{1,0:T(8,128)(2,1)S(1)} %collective-permute-done.6, ...), kind=kOutput, calls=%fused_computation.49 | convolution fusion | flops 36208640 | bytes 3997952 | tf_op jit(solution)/shard_map/dot_general | solution.py:86
  80.4 0.6 fusion.58
  81.0 1.7 %fusion.55 = (bf16[768,512]{1,0:T(8,128)(2,1)S(1)}, f32[768,512]{1,0:T(8,128)}) fusion(f32[768,512]{1,0:T(8,128)S(1)} %fusion.58, bf16[512,768]{0,1:T(8,128)(2,1)S(1)} %copy-done.1, bf16[512,512]{1,0:T(8,128)(2,1)S(1)} %fusion.25), kind=kOutput, calls=%fused_computation.86 | convolution fusion | flops 403439616 | bytes 5242880 | tf_op jit(solution)/shard_map/dot_general | solution.py:68
  82.7 0.7 fusion.49
  83.5 4.4 %collective-permute-start.9 = (bf16[128,512]{1,0:T(8,128)(2,1)}, bf16[128,512]{1,0:T(8,128)(2,1)S(1)}, u32[]{:S(2)}, u32[]{:S(2)}) collective-permute-start(bf16[128,512]{1,0:T(8,128)(2,1)} %get-tuple-element.5), channel_id=1, source_target_pairs={{0,15},{1,0},{2,1},{3,2},{4,3},{5,4},{6,5},{7,6},{8,7},{9,8},{10,9... | collective-permute-start | bytes 393224 | tf_op jit(solution)/shard_map/ppermute | solution.py:11
  87.9 0.2 fusion.6
  88.1 9.5 %all_to_all.31 = bf16[16,4,512]{2,1,0:T(4,128)(2,1)S(1)} all-to-all(bf16[16,4,512]{2,1,0:T(4,128)(2,1)S(1)} %reshape.59), channel_id=1, replica_groups=mesh['groups'=2,'graph'=16] {'graph'}, dimensions={0} | all-to-all | bytes 131072 | tf_op jit(solution)/shard_map/all_to_all | solution.py:78
  97.7 2.3 %fusion.26 = bf16[512,512]{1,0:T(8,128)(2,1)S(1)} fusion(f32[512,512]{1,0:T(8,128)} %get-tuple-element.15, s32[512,512]{1,0:T(8,128)} %param.12, f32[768,512]{1,0:T(8,128)} %get-tuple-element.19, bf16[128,512]{1,0:T(8,128)(2,1)S(1)} %collective-permute-done.9, bf16[128,512]{1,0:T(8,128)(2,1)S(1)} %collective-permute-done.8, ...), kind=kOutput, calls=%fused_computation.50 | convolution fusion | flops 36208640 | bytes 3997952 | tf_op jit(solution)/shard_map/dot_general | solution.py:86
  99.9 0.6 fusion.59
  100.5 1.7 %fusion.56 = (bf16[768,512]{1,0:T(8,128)(2,1)S(1)}, f32[768,512]{1,0:T(8,128)}) fusion(f32[768,512]{1,0:T(8,128)S(1)} %fusion.59, bf16[512,768]{0,1:T(8,128)(2,1)S(1)} %copy-done.1, bf16[512,512]{1,0:T(8,128)(2,1)S(1)} %fusion.26), kind=kOutput, calls=%fused_computation.87 | convolution fusion | flops 403439616 | bytes 5242880 | tf_op jit(solution)/shard_map/dot_general | solution.py:68
  102.2 0.7 fusion.48
  103.0 4.4 %collective-permute-start.11 = (bf16[128,512]{1,0:T(8,128)(2,1)}, bf16[128,512]{1,0:T(8,128)(2,1)S(1)}, u32[]{:S(2)}, u32[]{:S(2)}) collective-permute-start(bf16[128,512]{1,0:T(8,128)(2,1)} %get-tuple-element.3), channel_id=1, source_target_pairs={{0,15},{1,0},{2,1},{3,2},{4,3},{5,4},{6,5},{7,6},{8,7},{9,8},{10,9... | collective-permute-start | bytes 393224 | tf_op jit(solution)/shard_map/ppermute | solution.py:11
  107.4 0.2 fusion.7
  107.7 9.5 %all_to_all.32 = bf16[16,4,512]{2,1,0:T(4,128)(2,1)S(1)} all-to-all(bf16[16,4,512]{2,1,0:T(4,128)(2,1)S(1)} %reshape.61), channel_id=1, replica_groups=mesh['groups'=2,'graph'=16] {'graph'}, dimensions={0} | all-to-all | bytes 131072 | tf_op jit(solution)/shard_map/all_to_all | solution.py:78
  117.2 2.0 %fusion.12 = f32[512]{0:T(512)S(1)} fusion(f32[512,512]{1,0:T(8,128)} %get-tuple-element.15, f32[768,512]{1,0:T(8,128)S(1)} %copy-done.2, s32[512,512]{1,0:T(8,128)} %param.12, bf16[128,512]{1,0:T(8,128)(2,1)S(1)} %collective-permute-done.11, bf16[128,512]{1,0:T(8,128)(2,1)S(1)} %collective-permute-done.10, bf16[64,512]{1,0:T(8,128)(2,1)S(1)} %reshape.62, ...), kind=kOutput, calls=%fused_computation.33 | convolution fusion | flops 35945984 | bytes 3475712 | tf_op jit(solution)/shard_map/dot_general | solution.py:86
  119.1 0.6 broadcast_multiply_fusion
  (42 shorter events, 0.3 us)
Async XLA Ops:
  0.6 15.8 %copy-start = (bf16[4,8,128,128]{3,2,1,0:T(8,128)(2,1)S(1)}, bf16[4,8,128,128]{3,2,1,0:T(8,128)(2,1)}, u32[]{:S(2)}) copy-start(bf16[4,8,128,128]{3,2,1,0:T(8,128)(2,1)} %param.7) | copy-start | bytes 3145732
  0.6 15.7 %copy-start.8 = (s32[4,8]{1,0:T(4,128)S(1)}, s32[4,8]{1,0:T(4,128)}, u32[]{:S(2)}) copy-start(s32[4,8]{1,0:T(4,128)} %param.8) | copy-start | bytes 388
  2.9 15.7 %copy-start.3 = (bf16[512,512]{1,0:T(8,128)(2,1)}, bf16[512,512]{1,0:T(8,128)(2,1)S(1)}, u32[]{:S(2)}) copy-start(bf16[512,512]{1,0:T(8,128)(2,1)S(1)} %convert_element_type.83) | copy-start | bytes 1572868
  3.8 18.0 %all-to-all-start = ((bf16[16,4,512]{2,1,0:T(4,128)(2,1)}), bf16[16,4,512]{2,1,0:T(4,128)(2,1)S(1)}, u32[]{:S(2)}, u32[]{:S(2)}) async-start(bf16[16,4,512]{2,1,0:T(4,128)(2,1)} %reshape.51), calls=%async_computation | async-start | bytes 131072 | tf_op jit(solution)/shard_map/all_to_all | solution.py:53
  11.9 10.2 %collective-permute-start = (bf16[128,512]{1,0:T(8,128)(2,1)}, bf16[128,512]{1,0:T(8,128)(2,1)}, u32[]{:S(2)}, u32[]{:S(2)}) collective-permute-start(bf16[128,512]{1,0:T(8,128)(2,1)} %get-tuple-element.12), channel_id=1, source_target_pairs={{0,1},{1,2},{2,3},{3,4},{4,5},{5,6},{6,7},{7,8},{8,9},{9,10},{10,1... | collective-permute-start | bytes 393224 | tf_op jit(solution)/shard_map/ppermute | solution.py:11
  12.3 9.8 %collective-permute-start.1 = (bf16[128,512]{1,0:T(8,128)(2,1)}, bf16[128,512]{1,0:T(8,128)(2,1)}, u32[]{:S(2)}, u32[]{:S(2)}) collective-permute-start(bf16[128,512]{1,0:T(8,128)(2,1)} %get-tuple-element.13), channel_id=1, source_target_pairs={{0,15},{1,0},{2,1},{3,2},{4,3},{5,4},{6,5},{7,6},{8,7},{9,8},{10,9... | collective-permute-start | bytes 393224 | tf_op jit(solution)/shard_map/ppermute | solution.py:11
  20.6 1.2 copy-start.5
  22.1 2.0 %copy-start.4 = (bf16[512,512]{1,0:T(8,128)(2,1)S(1)}, bf16[512,512]{1,0:T(8,128)(2,1)}, u32[]{:S(2)}) copy-start(bf16[512,512]{1,0:T(8,128)(2,1)} %copy-done.3) | copy-start | bytes 1572868
  22.1 2.0 %copy-start.9 = (s32[512]{0:T(512)S(1)}, s32[512]{0:T(512)}, u32[]{:S(2)}) copy-start(s32[512]{0:T(512)} %param.11) | copy-start | bytes 6148
  25.8 12.8 %copy-start.6 = (bf16[512,512]{1,0:T(8,128)(2,1)}, bf16[512,512]{1,0:T(8,128)(2,1)S(1)}, u32[]{:S(2)}) copy-start(bf16[512,512]{1,0:T(8,128)(2,1)S(1)} %fusion.3) | copy-start | bytes 1572868
  25.8 12.8 %copy-start.1 = (bf16[512,768]{0,1:T(8,128)(2,1)S(1)}, bf16[512,768]{0,1:T(8,128)(2,1)}, u32[]{:S(2)}) copy-start(bf16[512,768]{0,1:T(8,128)(2,1)} %subtract_convert_fusion) | copy-start | bytes 2359300
  26.7 10.6 %all-to-all-start.1 = ((bf16[16,4,512]{2,1,0:T(4,128)(2,1)}), bf16[16,4,512]{2,1,0:T(4,128)(2,1)S(1)}, u32[]{:S(2)}, u32[]{:S(2)}) async-start(bf16[16,4,512]{2,1,0:T(4,128)(2,1)} %reshape.53), calls=%async_computation.1 | async-start | bytes 131072 | tf_op jit(solution)/shard_map/all_to_all | solution.py:53
  30.9 7.7 %collective-permute-start.2 = (bf16[128,512]{1,0:T(8,128)(2,1)}, bf16[128,512]{1,0:T(8,128)(2,1)}, u32[]{:S(2)}, u32[]{:S(2)}) collective-permute-start(bf16[128,512]{1,0:T(8,128)(2,1)} %get-tuple-element.10), channel_id=1, source_target_pairs={{0,1},{1,2},{2,3},{3,4},{4,5},{5,6},{6,7},{7,8},{8,9},{9,10},{10,1... | collective-permute-start | bytes 393224 | tf_op jit(solution)/shard_map/ppermute | solution.py:11
  31.2 7.4 %collective-permute-start.3 = (bf16[128,512]{1,0:T(8,128)(2,1)S(1)}, bf16[128,512]{1,0:T(8,128)(2,1)}, u32[]{:S(2)}, u32[]{:S(2)}) collective-permute-start(bf16[128,512]{1,0:T(8,128)(2,1)S(1)} %get-tuple-element.11), channel_id=1, source_target_pairs={{0,15},{1,0},{2,1},{3,2},{4,3},{5,4},{6,5},{7,6},{8,7},{9,8},{10,9... | collective-permute-start | bytes 393224 | tf_op jit(solution)/shard_map/ppermute | solution.py:11
  42.9 12.5 %all-to-all-start.2 = ((bf16[16,4,512]{2,1,0:T(4,128)(2,1)}), bf16[16,4,512]{2,1,0:T(4,128)(2,1)S(1)}, u32[]{:S(2)}, u32[]{:S(2)}) async-start(bf16[16,4,512]{2,1,0:T(4,128)(2,1)} %reshape.55), calls=%async_computation.2 | async-start | bytes 131072 | tf_op jit(solution)/shard_map/all_to_all | solution.py:53
  48.9 7.7 %collective-permute-start.4 = (bf16[128,512]{1,0:T(8,128)(2,1)}, bf16[128,512]{1,0:T(8,128)(2,1)}, u32[]{:S(2)}, u32[]{:S(2)}) collective-permute-start(bf16[128,512]{1,0:T(8,128)(2,1)} %get-tuple-element.8), channel_id=1, source_target_pairs={{0,1},{1,2},{2,3},{3,4},{4,5},{5,6},{6,7},{7,8},{8,9},{9,10},{10,1... | collective-permute-start | bytes 393224 | tf_op jit(solution)/shard_map/ppermute | solution.py:11
  49.3 7.3 %collective-permute-start.5 = (bf16[128,512]{1,0:T(8,128)(2,1)S(1)}, bf16[128,512]{1,0:T(8,128)(2,1)}, u32[]{:S(2)}, u32[]{:S(2)}) collective-permute-start(bf16[128,512]{1,0:T(8,128)(2,1)S(1)} %get-tuple-element.9), channel_id=1, source_target_pairs={{0,15},{1,0},{2,1},{3,2},{4,3},{5,4},{6,5},{7,6},{8,7},{9,8},{10,9... | collective-permute-start | bytes 393224 | tf_op jit(solution)/shard_map/ppermute | solution.py:11
  55.8 2.4 %copy-start.7 = (s32[512,512]{1,0:T(8,128)S(1)}, s32[512,512]{1,0:T(8,128)}, u32[]{:S(2)}) copy-start(s32[512,512]{1,0:T(8,128)} %param.12) | copy-start | bytes 3145732
  63.9 14.2 %collective-permute-start.6 = (bf16[128,512]{1,0:T(8,128)(2,1)}, bf16[128,512]{1,0:T(8,128)(2,1)S(1)}, u32[]{:S(2)}, u32[]{:S(2)}) collective-permute-start(bf16[128,512]{1,0:T(8,128)(2,1)} %get-tuple-element.6), channel_id=1, source_target_pairs={{0,1},{1,2},{2,3},{3,4},{4,5},{5,6},{6,7},{7,8},{8,9},{9,10},{10,1... | collective-permute-start | bytes 393224 | tf_op jit(solution)/shard_map/ppermute | solution.py:11
  64.3 13.8 %collective-permute-start.7 = (bf16[128,512]{1,0:T(8,128)(2,1)}, bf16[128,512]{1,0:T(8,128)(2,1)S(1)}, u32[]{:S(2)}, u32[]{:S(2)}) collective-permute-start(bf16[128,512]{1,0:T(8,128)(2,1)} %get-tuple-element.7), channel_id=1, source_target_pairs={{0,15},{1,0},{2,1},{3,2},{4,3},{5,4},{6,5},{7,6},{8,7},{9,8},{10,9... | collective-permute-start | bytes 393224 | tf_op jit(solution)/shard_map/ppermute | solution.py:11
  83.5 14.2 %collective-permute-start.8 = (bf16[128,512]{1,0:T(8,128)(2,1)}, bf16[128,512]{1,0:T(8,128)(2,1)S(1)}, u32[]{:S(2)}, u32[]{:S(2)}) collective-permute-start(bf16[128,512]{1,0:T(8,128)(2,1)} %get-tuple-element.4), channel_id=1, source_target_pairs={{0,1},{1,2},{2,3},{3,4},{4,5},{5,6},{6,7},{7,8},{8,9},{9,10},{10,1... | collective-permute-start | bytes 393224 | tf_op jit(solution)/shard_map/ppermute | solution.py:11
  83.5 14.2 %collective-permute-start.9 = (bf16[128,512]{1,0:T(8,128)(2,1)}, bf16[128,512]{1,0:T(8,128)(2,1)S(1)}, u32[]{:S(2)}, u32[]{:S(2)}) collective-permute-start(bf16[128,512]{1,0:T(8,128)(2,1)} %get-tuple-element.5), channel_id=1, source_target_pairs={{0,15},{1,0},{2,1},{3,2},{4,3},{5,4},{6,5},{7,6},{8,7},{9,8},{10,9... | collective-permute-start | bytes 393224 | tf_op jit(solution)/shard_map/ppermute | solution.py:11
  102.2 14.9 %copy-start.2 = (f32[768,512]{1,0:T(8,128)S(1)}, f32[768,512]{1,0:T(8,128)}, u32[]{:S(2)}) copy-start(f32[768,512]{1,0:T(8,128)} %get-tuple-element.21) | copy-start | bytes 4718596
  103.0 14.2 %collective-permute-start.10 = (bf16[128,512]{1,0:T(8,128)(2,1)}, bf16[128,512]{1,0:T(8,128)(2,1)S(1)}, u32[]{:S(2)}, u32[]{:S(2)}) collective-permute-start(bf16[128,512]{1,0:T(8,128)(2,1)} %get-tuple-element.2), channel_id=1, source_target_pairs={{0,1},{1,2},{2,3},{3,4},{4,5},{5,6},{6,7},{7,8},{8,9},{9,10},{10,1... | collective-permute-start | bytes 393224 | tf_op jit(solution)/shard_map/ppermute | solution.py:11
  103.0 14.2 %collective-permute-start.11 = (bf16[128,512]{1,0:T(8,128)(2,1)}, bf16[128,512]{1,0:T(8,128)(2,1)S(1)}, u32[]{:S(2)}, u32[]{:S(2)}) collective-permute-start(bf16[128,512]{1,0:T(8,128)(2,1)} %get-tuple-element.3), channel_id=1, source_target_pairs={{0,15},{1,0},{2,1},{3,2},{4,3},{5,4},{6,5},{7,6},{8,7},{9,8},{10,9... | collective-permute-start | bytes 393224 | tf_op jit(solution)/shard_map/ppermute | solution.py:11

commit v2 on v1

--- a/solution.py
+++ b/solution.py
@@ -35,46 +35,48 @@
     dense = jnp.einsum("tks,tkij->tisj", tile_pick, tile_weight, preferred_element_type=jnp.float32)
     dense = dense.reshape(links_here, span * tile_size)
     w_high, w_low = split_high_low(dense)
-    wt_high = w_high.T
-    wt_low = w_low.T
     send_flat = send_rows.reshape(-1)
     row_pick = (jnp.arange(links_here, dtype=jnp.int32)[:, None] == send_flat[None, :]).astype(
         jnp.bfloat16
     )
-    row_pick_t = row_pick.T
+    peers = send_rows.shape[0]
+    row_pick3 = row_pick.reshape(links_here, peers, slot_count)
+    far_weight3 = far_weight.reshape(links_here, peers, slot_count)
+    far_slots = far_weight.shape[1]
+    w_value = jnp.concatenate([w_high, w_low], axis=1)
+    w_load = jnp.concatenate([w_high.T, w_low.T], axis=1)
 
     values = values_start
     for sweep_idx in range(SWEEPS):
         narrow = values.astype(jnp.bfloat16)
         head = narrow[:tile_size]
         tail = narrow[links_here - tile_size :]
-        outgoing = jnp.dot(row_pick_t, narrow, preferred_element_type=jnp.float32).astype(jnp.bfloat16)
-        outgoing = outgoing.reshape(peer_count, slot_count, dest_count)
+        outgoing = jnp.einsum(
+            "lps,ld->psd", row_pick3, narrow, preferred_element_type=jnp.float32
+        ).astype(jnp.bfloat16)
         received = lax.all_to_all(outgoing, "graph", split_axis=0, concat_axis=0, tiled=True)
         from_prev = passed_along(tail, "graph", 1)
         from_next = passed_along(head, "graph", -1)
-        padded = jnp.concatenate([from_prev, narrow, from_next], axis=0)
-        near = jnp.dot(w_high, padded, preferred_element_type=jnp.float32) + jnp.dot(
-            w_low, padded, preferred_element_type=jnp.float32
+        stacked = jnp.concatenate(
+            [from_prev, narrow, from_next, from_prev, narrow, from_next], axis=0
         )
-        flat = received.reshape(-1, dest_count)
-        far = jnp.dot(far_weight, flat, preferred_element_type=jnp.float32)
-        values = near + far + dest_mask
+        far = jnp.einsum("lps,psd->ld", far_weight3, received, preferred_element_type=jnp.float32)
+        values = jnp.dot(w_value, stacked, preferred_element_type=jnp.float32) + far + dest_mask
 
     load = demand_flow
     rest_rows = links_here - tile_size
+    span_rows = span * tile_size
     for sweep_idx in range(SWEEPS):
         ratio = (load / values).astype(jnp.bfloat16)
-        landed = jnp.dot(wt_high, ratio, preferred_element_type=jnp.float32) + jnp.dot(
-            wt_low, ratio, preferred_element_type=jnp.float32
+        landed = jnp.dot(
+            w_load, jnp.concatenate([ratio, ratio], axis=0), preferred_element_type=jnp.float32
         )
         lower_rim = landed[:tile_size].astype(jnp.bfloat16)
-        upper_rim = landed[tile_size + links_here :].astype(jnp.bfloat16)
+        upper_rim = landed[tile_size + links_here : span_rows].astype(jnp.bfloat16)
         own_part = landed[tile_size : tile_size + links_here]
-        far_part = lax.dot_general(
-            far_weight, ratio, (((0,), (0,)), ((), ())), preferred_element_type=jnp.float32
-        )
-        far_part = far_part.astype(jnp.bfloat16).reshape(peer_count, slot_count, dest_count)
+        far_part = jnp.einsum(
+            "lps,ld->psd", far_weight3, ratio, preferred_element_type=jnp.float32
+        ).astype(jnp.bfloat16)
         returned = lax.all_to_all(far_part, "graph", split_axis=0, concat_axis=0, tiled=True)
         from_next = passed_along(lower_rim, "graph", -1).astype(jnp.float32)
         from_prev = passed_along(upper_rim, "graph", 1).astype(jnp.float32)
@@ -83,7 +85,7 @@
             + jnp.pad(from_prev, ((0, rest_rows), (0, 0)))
             + jnp.pad(from_next, ((rest_rows, 0), (0, 0)))
         )
-        far_in = jnp.dot(row_pick, returned.reshape(-1, dest_count), preferred_element_type=jnp.float32)
+        far_in = jnp.einsum("lps,psd->ld", row_pick3, returned, preferred_element_type=jnp.float32)
         load = values * (own_part + far_in) + demand_flow
     flows = jnp.mean(load, axis=1)
     return (values, flows)

time: 120 us -> 105 us (0.88)
  matrix products: 27.7 us -> 11.8 us
  waiting for transfers between devices: 5.82 us -> 7.32 us
    dot_general x24 -> x18, matrix products: 27 us -> 11.1 us  [the longest x3 3.17 us: shards(): jnp.dot(w_value, stacked, preferred_element_type=jnp.float32) + far]
    slice x6, local copies, waits for them, and re-layouts: 4.3 us -> 0.84 us  [the longest x3 0.78 us: shards(): head = narrow[:tile_size]]
    all_to_all x3, starting transfers between devices: 16.2 us -> 13.7 us  [shards(): lax.all_to_all(outgoing, 'graph', split_axis=0, concat_axis=0, tiled=True)]
    all_to_all x3, waiting for transfers between devices: 4.14 us -> 6.36 us  [shards(): lax.all_to_all(outgoing, 'graph', split_axis=0, concat_axis=0, tiled=True)]
    convert_element_type x0 -> x6, local copies, waits for them, and re-layouts: none -> 2.17 us  [the longest x3 2.01 us: shards(): outgoing = jnp.einsum('lps,ld->psd', row_pick3, narrow, preferred_element...]
    unnamed x22 -> x34, local copies, waits for them, and re-layouts: 2.43 us -> 4.07 us
    ppermute x12, starting transfers between devices: 26.7 us -> 27.9 us  [passed_along(): lax.ppermute(value, axis, [(source, (source + steps) % count) for source...]
  transfers between devices with their start and end apart: 15 -> 15, of which waited for: 4 -> 5; matrix products, arithmetic and copies ran while one was open for 8% -> 10% of each run, Pallas kernels for 0% -> 0%
where the time goes in v2:
time: 105 us; the launch traced here: 104 us
  starting transfers between devices  41.6 us (40%)
  blocking collectives  28.4 us (27%)
  matrix products  11.8 us (11%)
  local copies, waits for them, and re-layouts  10.8 us (10%)
  waiting for transfers between devices  7.32 us (7%)
  other arithmetic  3.34 us (3%)
  between operations  1.18 us (1%)
    all_to_all x3, blocking collectives, shards(): lax.all_to_all(far_part, 'graph', split_axis=0, concat_axis=0, tiled=True)  28.4 us
    ppermute x12, starting transfers between devices, passed_along(): lax.ppermute(value, axis, [(source, (source + steps) % count) for source...  27.9 us
    all_to_all x3, starting transfers between devices, shards(): lax.all_to_all(outgoing, 'graph', split_axis=0, concat_axis=0, tiled=True)  13.7 us
    all_to_all x3, waiting for transfers between devices, shards(): lax.all_to_all(outgoing, 'graph', split_axis=0, concat_axis=0, tiled=True)  6.36 us
    unnamed x34, local copies, waits for them, and re-layouts  4.07 us
    dot_general x3, matrix products, shards(): jnp.dot(w_value, stacked, preferred_element_type=jnp.float32) + far  3.17 us
    dot_general x3, matrix products, shards(): jnp.dot(w_load, jnp.concatenate([ratio, ratio], axis=0), preferred_elemen...  2.91 us
  transfers between devices with their start and end apart: 15, of which 5 were waited for; matrix products, arithmetic and copies ran while one was open for 10% of the time, Pallas kernels for 0%

profile of v2, /device:TPU:0, one launch (start us, length us, event | category | flops | bytes accessed | tf_op | source)
XLA Modules:
  0.0 104.4 jit_solution(6850416066770708987)
XLA Ops:
  0.6 0.0 copy-start
  0.7 1.4 %convert_element_type.85 = bf16[512,512]{1,0:T(8,128)(2,1)S(1)} convert(f32[512,512]{1,0:T(8,128)} %param.13) | non-fusion elementwise | flops 262144 | bytes 1572864 | tf_op jit(solution)/shard_map/convert_element_type | solution.py:51
  2.0 0.7 fusion.74
  2.8 0.5 collective-permute-start
  3.3 5.0 %collective-permute-start.1 = (bf16[128,512]{1,0:T(8,128)(2,1)}, bf16[128,512]{1,0:T(8,128)(2,1)}, u32[]{:S(2)}, u32[]{:S(2)}) collective-permute-start(bf16[128,512]{1,0:T(8,128)(2,1)} %get-tuple-element.12), channel_id=1, source_target_pairs={{0,15},{1,0},{2,1},{3,2},{4,3},{5,4},{6,5},{7,6},{8,7},{9,8},{10,9... | collective-permute-start | bytes 393224 | tf_op jit(solution)/shard_map/ppermute | solution.py:11
  8.2 0.2 convolution_convert_fusion.5
  8.5 0.7 copy.26
  9.1 4.1 %all-to-all-start = ((bf16[16,4,512]{2,1,0:T(4,128)(2,1)}), bf16[16,4,512]{2,1,0:T(4,128)(2,1)}, u32[]{:S(2)}, u32[]{:S(2)}) async-start(bf16[16,4,512]{2,1,0:T(4,128)(2,1)} %copy.26), calls=%async_computation | async-start | bytes 131072 | tf_op jit(solution)/shard_map/all_to_all | solution.py:57
  13.3 0.7 fusion.32
  14.0 1.5 %copy.80 = f32[64,8,6,128]{3,1,2,0:T(8,128)} copy(f32[64,8,6,128]{3,2,1,0:T(8,128)S(1)} %bitcast.66) | data formatting | bytes 3145728
  15.6 1.9 %copy.50 = f32[512,768]{0,1:T(8,128)S(1)} copy(f32[512,768]{1,0:T(8,128)} %bitcast.67) | data formatting | bytes 3145728 | tf_op jit(solution)/shard_map/reshape | solution.py:36
  17.4 0.1 convert_element_type.82
  17.5 1.1 %subtract_convert_fusion = bf16[512,768]{0,1:T(8,128)(2,1)} fusion(f32[512,768]{0,1:T(8,128)S(1)} %copy.50, bf16[512,768]{0,1:T(8,128)(2,1)S(1)} %convert_element_type.82), kind=kLoop, calls=%fused_computation.6 | loop fusion | flops 1179648 | bytes 3145728 | tf_op jit(solution)/shard_map/convert_element_type | solution.py:16
  18.7 0.9 reshape.27
  19.6 0.6 all-to-all-done
  20.2 1.2 %convolution_bitcast_fusion.5 = f32[512,512]{1,0:T(8,128)S(1)} fusion(bf16[16,4,512]{2,1,0:T(4,128)(2,1)} %all-to-all-done, bf16[512,16,4]{0,2,1:T(4,128)(2,1)S(1)} %reshape.27), kind=kOutput, calls=%fused_computation.12 | convolution fusion | flops 33554432 | bytes 1179648 | tf_op jit(solution)/shard_map/lps,psd->ld/dot_general | solution.py:63
  21.4 0.1 constant_dynamic-update-slice_fusion.4
  21.5 1.0 constant_dynamic-update-slice_fusion.3
  22.5 0.1 constant_dynamic-update-slice_fusion.1
  22.6 0.9 constant_dynamic-update-slice_fusion
  23.5 1.0 fusion
  24.6 0.2 convolution_convert_fusion.4
  24.8 0.7 copy.29
  25.5 5.4 %all-to-all-start.1 = ((bf16[16,4,512]{2,1,0:T(4,128)(2,1)}), bf16[16,4,512]{2,1,0:T(4,128)(2,1)S(1)}, u32[]{:S(2)}, u32[]{:S(2)}) async-start(bf16[16,4,512]{2,1,0:T(4,128)(2,1)} %copy.29), calls=%async_computation.1 | async-start | bytes 131072 | tf_op jit(solution)/shard_map/all_to_all | solution.py:57
  30.9 0.5 collective-permute-start.2
  31.3 4.0 %collective-permute-start.3 = (bf16[128,512]{1,0:T(8,128)(2,1)S(1)}, bf16[128,512]{1,0:T(8,128)(2,1)S(1)}, u32[]{:S(2)}, u32[]{:S(2)}) collective-permute-start(bf16[128,512]{1,0:T(8,128)(2,1)S(1)} %get-tuple-element.10), channel_id=1, source_target_pairs={{0,15},{1,0},{2,1},{3,2},{4,3},{5,4},{6,5},{7,6},{8,7},{9,8},{10,9... | collective-permute-start | bytes 393224 | tf_op jit(solution)/shard_map/ppermute | solution.py:11
  35.4 2.9 %all-to-all-done.1 = bf16[16,4,512]{2,1,0:T(4,128)(2,1)S(1)} async-done(((bf16[16,4,512]{2,1,0:T(4,128)(2,1)}), bf16[16,4,512]{2,1,0:T(4,128)(2,1)S(1)}, u32[]{:S(2)}, u32[]{:S(2)}) %all-to-all-start.1) | async-done | bytes 65568 | tf_op jit(solution)/shard_map/all_to_all | solution.py:57
  38.3 0.3 convolution_bitcast_fusion.4
  38.6 0.5 collective-permute-done.2
  39.3 0.5 copy-done.5
  39.8 1.0 fusion.1
  40.8 0.2 convolution_convert_fusion.3
  41.0 0.7 copy.32
  41.7 4.2 %all-to-all-start.2 = ((bf16[16,4,512]{2,1,0:T(4,128)(2,1)}), bf16[16,4,512]{2,1,0:T(4,128)(2,1)S(1)}, u32[]{:S(2)}, u32[]{:S(2)}) async-start(bf16[16,4,512]{2,1,0:T(4,128)(2,1)} %copy.32), calls=%async_computation.2 | async-start | bytes 131072 | tf_op jit(solution)/shard_map/all_to_all | solution.py:57
  45.9 0.5 collective-permute-start.4
  46.4 4.0 %collective-permute-start.5 = (bf16[128,512]{1,0:T(8,128)(2,1)S(1)}, bf16[128,512]{1,0:T(8,128)(2,1)S(1)}, u32[]{:S(2)}, u32[]{:S(2)}) collective-permute-start(bf16[128,512]{1,0:T(8,128)(2,1)S(1)} %get-tuple-element.8), channel_id=1, source_target_pairs={{0,15},{1,0},{2,1},{3,2},{4,3},{5,4},{6,5},{7,6},{8,7},{9,8},{10,9... | collective-permute-start | bytes 393224 | tf_op jit(solution)/shard_map/ppermute | solution.py:11
  50.4 2.9 %all-to-all-done.2 = bf16[16,4,512]{2,1,0:T(4,128)(2,1)S(1)} async-done(((bf16[16,4,512]{2,1,0:T(4,128)(2,1)}), bf16[16,4,512]{2,1,0:T(4,128)(2,1)S(1)}, u32[]{:S(2)}, u32[]{:S(2)}) %all-to-all-start.2) | async-done | bytes 65568 | tf_op jit(solution)/shard_map/all_to_all | solution.py:57
  53.3 0.3 convolution_bitcast_fusion.3
  53.7 0.5 collective-permute-done.4
  54.3 0.6 copy-done.2
  54.9 0.2 copy-done.6
  55.1 1.1 %divide_convert_fusion = (bf16[512,512]{1,0:T(8,128)(2,1)S(1)}, f32[512,512]{1,0:T(8,128)S(1)}) fusion(s32[512,512]{1,0:T(8,128)S(1)} %copy-done.2, s32[512]{0:T(512)S(1)} %copy-done.9, s32[512]{0:T(512)S(1)} %iota_add_fusion, f32[512,512]{1,0:T(8,128)S(1)} %convolution_bitcast_fusion.3, bf16[1536,512]{1,0:T(8,128)(2,1)S(1)} %constant_dynamic-update-slice_fusion.12, ...), kind=kOutput, calls=%fused_computation.59 | convolution fusion | flops 810287104 | bytes 6819840 | tf_op jit(solution)/shard_map/dot_general | solution.py:64
  56.3 1.0 fusion.75
  57.3 0.1 collective-permute-start.6
  57.4 4.4 %collective-permute-start.7 = (bf16[128,512]{1,0:T(8,128)(2,1)S(1)}, bf16[128,512]{1,0:T(8,128)(2,1)S(1)}, u32[]{:S(2)}, u32[]{:S(2)}) collective-permute-start(bf16[128,512]{1,0:T(8,128)(2,1)S(1)} %get-tuple-element.7), channel_id=1, source_target_pairs={{0,15},{1,0},{2,1},{3,2},{4,3},{5,4},{6,5},{7,6},{8,7},{9,8},{10,9... | collective-permute-start | bytes 393224 | tf_op jit(solution)/shard_map/ppermute | solution.py:11
  61.8 0.2 fusion.2
  62.0 0.1 copy.36
  62.1 9.5 %all_to_all.30 = bf16[16,4,512]{2,1,0:T(4,128)(2,1)S(1)} all-to-all(bf16[16,4,512]{2,1,0:T(4,128)(2,1)S(1)} %copy.36), channel_id=1, replica_groups=mesh['groups'=2,'graph'=16] {'graph'}, dimensions={0} | all-to-all | bytes 131072 | tf_op jit(solution)/shard_map/all_to_all | solution.py:80
  71.5 0.6 fusion.34
  72.1 1.0 fusion.76
  73.1 0.1 collective-permute-start.8
  73.2 4.4 %collective-permute-start.9 = (bf16[128,512]{1,0:T(8,128)(2,1)S(1)}, bf16[128,512]{1,0:T(8,128)(2,1)S(1)}, u32[]{:S(2)}, u32[]{:S(2)}) collective-permute-start(bf16[128,512]{1,0:T(8,128)(2,1)S(1)} %get-tuple-element.5), channel_id=1, source_target_pairs={{0,15},{1,0},{2,1},{3,2},{4,3},{5,4},{6,5},{7,6},{8,7},{9,8},{10,9... | collective-permute-start | bytes 393224 | tf_op jit(solution)/shard_map/ppermute | solution.py:11
  77.6 0.2 fusion.3
  77.8 0.1 copy.39
  77.9 9.5 %all_to_all.31 = bf16[16,4,512]{2,1,0:T(4,128)(2,1)S(1)} all-to-all(bf16[16,4,512]{2,1,0:T(4,128)(2,1)S(1)} %copy.39), channel_id=1, replica_groups=mesh['groups'=2,'graph'=16] {'graph'}, dimensions={0} | all-to-all | bytes 131072 | tf_op jit(solution)/shard_map/all_to_all | solution.py:80
  87.4 0.6 fusion.35
  88.0 1.0 fusion.77
  89.0 0.1 collective-permute-start.10
  89.0 4.4 %collective-permute-start.11 = (bf16[128,512]{1,0:T(8,128)(2,1)S(1)}, bf16[128,512]{1,0:T(8,128)(2,1)S(1)}, u32[]{:S(2)}, u32[]{:S(2)}) collective-permute-start(bf16[128,512]{1,0:T(8,128)(2,1)S(1)} %get-tuple-element.3), channel_id=1, source_target_pairs={{0,15},{1,0},{2,1},{3,2},{4,3},{5,4},{6,5},{7,6},{8,7},{9,8},{10,9... | collective-permute-start | bytes 393224 | tf_op jit(solution)/shard_map/ppermute | solution.py:11
  93.5 0.2 fusion.4
  93.7 0.1 copy.44
  93.7 9.5 %all_to_all.32 = bf16[16,4,512]{2,1,0:T(4,128)(2,1)S(1)} all-to-all(bf16[16,4,512]{2,1,0:T(4,128)(2,1)S(1)} %copy.44), channel_id=1, replica_groups=mesh['groups'=2,'graph'=16] {'graph'}, dimensions={0} | all-to-all | bytes 131072 | tf_op jit(solution)/shard_map/all_to_all | solution.py:80
  103.2 0.6 fusion.9
  103.9 0.6 broadcast_multiply_fusion
  (47 shorter events, 0.4 us)
Async XLA Ops:
  0.6 12.7 %copy-start = (bf16[4,8,128,128]{3,2,1,0:T(8,128)(2,1)S(1)}, bf16[4,8,128,128]{3,2,1,0:T(8,128)(2,1)}, u32[]{:S(2)}) copy-start(bf16[4,8,128,128]{3,2,1,0:T(8,128)(2,1)} %param.7) | copy-start | bytes 3145732
  0.6 7.6 %copy-start.7 = (s32[16,4]{0,1:T(4,128)S(1)}, s32[16,4]{0,1:T(4,128)}, u32[]{:S(2)}) copy-start(s32[16,4]{0,1:T(4,128)} %param.10) | copy-start | bytes 772
  0.7 12.6 %copy-start.8 = (s32[4,8]{1,0:T(4,128)S(1)}, s32[4,8]{1,0:T(4,128)}, u32[]{:S(2)}) copy-start(s32[4,8]{1,0:T(4,128)} %param.8) | copy-start | bytes 388
  2.8 18.6 %collective-permute-start = (bf16[128,512]{1,0:T(8,128)(2,1)}, bf16[128,512]{1,0:T(8,128)(2,1)S(1)}, u32[]{:S(2)}, u32[]{:S(2)}) collective-permute-start(bf16[128,512]{1,0:T(8,128)(2,1)} %get-tuple-element.13), channel_id=1, source_target_pairs={{0,1},{1,2},{2,3},{3,4},{4,5},{5,6},{6,7},{7,8},{8,9},{9,10},{10,1... | collective-permute-start | bytes 393224 | tf_op jit(solution)/shard_map/ppermute | solution.py:11
  3.3 18.2 %collective-permute-start.1 = (bf16[128,512]{1,0:T(8,128)(2,1)}, bf16[128,512]{1,0:T(8,128)(2,1)}, u32[]{:S(2)}, u32[]{:S(2)}) collective-permute-start(bf16[128,512]{1,0:T(8,128)(2,1)} %get-tuple-element.12), channel_id=1, source_target_pairs={{0,15},{1,0},{2,1},{3,2},{4,3},{5,4},{6,5},{7,6},{8,7},{9,8},{10,9... | collective-permute-start | bytes 393224 | tf_op jit(solution)/shard_map/ppermute | solution.py:11
  9.1 11.0 %all-to-all-start = ((bf16[16,4,512]{2,1,0:T(4,128)(2,1)}), bf16[16,4,512]{2,1,0:T(4,128)(2,1)}, u32[]{:S(2)}, u32[]{:S(2)}) async-start(bf16[16,4,512]{2,1,0:T(4,128)(2,1)} %copy.26), calls=%async_computation | async-start | bytes 131072 | tf_op jit(solution)/shard_map/all_to_all | solution.py:57
  18.7 2.7 %copy-start.1 = (f32[512,512]{1,0:T(8,128)S(1)}, f32[512,512]{1,0:T(8,128)}, u32[]{:S(2)}) copy-start(f32[512,512]{1,0:T(8,128)} %param.13) | copy-start | bytes 3145732
  21.5 2.0 %copy-start.4 = (bf16[512,768]{0,1:T(8,128)(2,1)S(1)}, bf16[512,768]{0,1:T(8,128)(2,1)}, u32[]{:S(2)}) copy-start(bf16[512,768]{0,1:T(8,128)(2,1)} %subtract_convert_fusion) | copy-start | bytes 2359300
  21.5 2.0 %copy-start.9 = (s32[512]{0:T(512)S(1)}, s32[512]{0:T(512)}, u32[]{:S(2)}) copy-start(s32[512]{0:T(512)} %param.11) | copy-start | bytes 6148
  25.5 12.8 %all-to-all-start.1 = ((bf16[16,4,512]{2,1,0:T(4,128)(2,1)}), bf16[16,4,512]{2,1,0:T(4,128)(2,1)S(1)}, u32[]{:S(2)}, u32[]{:S(2)}) async-start(bf16[16,4,512]{2,1,0:T(4,128)(2,1)} %copy.29), calls=%async_computation.1 | async-start | bytes 131072 | tf_op jit(solution)/shard_map/all_to_all | solution.py:57
  30.9 8.2 %collective-permute-start.2 = (bf16[128,512]{1,0:T(8,128)(2,1)S(1)}, bf16[128,512]{1,0:T(8,128)(2,1)S(1)}, u32[]{:S(2)}, u32[]{:S(2)}) collective-permute-start(bf16[128,512]{1,0:T(8,128)(2,1)S(1)} %get-tuple-element.11), channel_id=1, source_target_pairs={{0,1},{1,2},{2,3},{3,4},{4,5},{5,6},{6,7},{7,8},{8,9},{9,10},{10,1... | collective-permute-start | bytes 393224 | tf_op jit(solution)/shard_map/ppermute | solution.py:11
  31.3 7.8 %collective-permute-start.3 = (bf16[128,512]{1,0:T(8,128)(2,1)S(1)}, bf16[128,512]{1,0:T(8,128)(2,1)S(1)}, u32[]{:S(2)}, u32[]{:S(2)}) collective-permute-start(bf16[128,512]{1,0:T(8,128)(2,1)S(1)} %get-tuple-element.10), channel_id=1, source_target_pairs={{0,15},{1,0},{2,1},{3,2},{4,3},{5,4},{6,5},{7,6},{8,7},{9,8},{10,9... | collective-permute-start | bytes 393224 | tf_op jit(solution)/shard_map/ppermute | solution.py:11
  38.6 1.1 %copy-start.5 = (bf16[512,768]{0,1:T(8,128)(2,1)S(1)}, bf16[512,768]{0,1:T(8,128)(2,1)}, u32[]{:S(2)}) copy-start(bf16[512,768]{0,1:T(8,128)(2,1)} %subtract_convert_fusion) | copy-start | bytes 2359300
  41.7 11.6 %all-to-all-start.2 = ((bf16[16,4,512]{2,1,0:T(4,128)(2,1)}), bf16[16,4,512]{2,1,0:T(4,128)(2,1)S(1)}, u32[]{:S(2)}, u32[]{:S(2)}) async-start(bf16[16,4,512]{2,1,0:T(4,128)(2,1)} %copy.32), calls=%async_computation.2 | async-start | bytes 131072 | tf_op jit(solution)/shard_map/all_to_all | solution.py:57
  45.9 8.2 %collective-permute-start.4 = (bf16[128,512]{1,0:T(8,128)(2,1)S(1)}, bf16[128,512]{1,0:T(8,128)(2,1)S(1)}, u32[]{:S(2)}, u32[]{:S(2)}) collective-permute-start(bf16[128,512]{1,0:T(8,128)(2,1)S(1)} %get-tuple-element.9), channel_id=1, source_target_pairs={{0,1},{1,2},{2,3},{3,4},{4,5},{5,6},{6,7},{7,8},{8,9},{9,10},{10,1... | collective-permute-start | bytes 393224 | tf_op jit(solution)/shard_map/ppermute | solution.py:11
  46.4 7.8 %collective-permute-start.5 = (bf16[128,512]{1,0:T(8,128)(2,1)S(1)}, bf16[128,512]{1,0:T(8,128)(2,1)S(1)}, u32[]{:S(2)}, u32[]{:S(2)}) collective-permute-start(bf16[128,512]{1,0:T(8,128)(2,1)S(1)} %get-tuple-element.8), channel_id=1, source_target_pairs={{0,15},{1,0},{2,1},{3,2},{4,3},{5,4},{6,5},{7,6},{8,7},{9,8},{10,9... | collective-permute-start | bytes 393224 | tf_op jit(solution)/shard_map/ppermute | solution.py:11
  53.7 1.2 %copy-start.2 = (s32[512,512]{1,0:T(8,128)S(1)}, s32[512,512]{1,0:T(8,128)}, u32[]{:S(2)}) copy-start(s32[512,512]{1,0:T(8,128)} %param.12) | copy-start | bytes 3145732
  53.7 1.4 %copy-start.6 = (bf16[512,768]{0,1:T(8,128)(2,1)S(1)}, bf16[512,768]{0,1:T(8,128)(2,1)}, u32[]{:S(2)}) copy-start(bf16[512,768]{0,1:T(8,128)(2,1)} %subtract_convert_fusion) | copy-start | bytes 2359300
  56.3 47.0 %copy-start.3 = (f32[512,512]{1,0:T(8,128)}, f32[512,512]{1,0:T(8,128)S(1)}, u32[]{:S(2)}) copy-start(f32[512,512]{1,0:T(8,128)S(1)} %get-tuple-element.15) | copy-start | bytes 3145732
  57.3 14.2 %collective-permute-start.6 = (bf16[128,512]{1,0:T(8,128)(2,1)S(1)}, bf16[128,512]{1,0:T(8,128)(2,1)S(1)}, u32[]{:S(2)}, u32[]{:S(2)}) collective-permute-start(bf16[128,512]{1,0:T(8,128)(2,1)S(1)} %get-tuple-element.6), channel_id=1, source_target_pairs={{0,1},{1,2},{2,3},{3,4},{4,5},{5,6},{6,7},{7,8},{8,9},{9,10},{10,1... | collective-permute-start | bytes 393224 | tf_op jit(solution)/shard_map/ppermute | solution.py:11
  57.4 14.2 %collective-permute-start.7 = (bf16[128,512]{1,0:T(8,128)(2,1)S(1)}, bf16[128,512]{1,0:T(8,128)(2,1)S(1)}, u32[]{:S(2)}, u32[]{:S(2)}) collective-permute-start(bf16[128,512]{1,0:T(8,128)(2,1)S(1)} %get-tuple-element.7), channel_id=1, source_target_pairs={{0,15},{1,0},{2,1},{3,2},{4,3},{5,4},{6,5},{7,6},{8,7},{9,8},{10,9... | collective-permute-start | bytes 393224 | tf_op jit(solution)/shard_map/ppermute | solution.py:11
  73.1 14.2 %collective-permute-start.8 = (bf16[128,512]{1,0:T(8,128)(2,1)S(1)}, bf16[128,512]{1,0:T(8,128)(2,1)S(1)}, u32[]{:S(2)}, u32[]{:S(2)}) collective-permute-start(bf16[128,512]{1,0:T(8,128)(2,1)S(1)} %get-tuple-element.4), channel_id=1, source_target_pairs={{0,1},{1,2},{2,3},{3,4},{4,5},{5,6},{6,7},{7,8},{8,9},{9,10},{10,1... | collective-permute-start | bytes 393224 | tf_op jit(solution)/shard_map/ppermute | solution.py:11
  73.2 14.2 %collective-permute-start.9 = (bf16[128,512]{1,0:T(8,128)(2,1)S(1)}, bf16[128,512]{1,0:T(8,128)(2,1)S(1)}, u32[]{:S(2)}, u32[]{:S(2)}) collective-permute-start(bf16[128,512]{1,0:T(8,128)(2,1)S(1)} %get-tuple-element.5), channel_id=1, source_target_pairs={{0,15},{1,0},{2,1},{3,2},{4,3},{5,4},{6,5},{7,6},{8,7},{9,8},{10,9... | collective-permute-start | bytes 393224 | tf_op jit(solution)/shard_map/ppermute | solution.py:11
  89.0 14.2 %collective-permute-start.10 = (bf16[128,512]{1,0:T(8,128)(2,1)S(1)}, bf16[128,512]{1,0:T(8,128)(2,1)S(1)}, u32[]{:S(2)}, u32[]{:S(2)}) collective-permute-start(bf16[128,512]{1,0:T(8,128)(2,1)S(1)} %get-tuple-element.2), channel_id=1, source_target_pairs={{0,1},{1,2},{2,3},{3,4},{4,5},{5,6},{6,7},{7,8},{8,9},{9,10},{10,1... | collective-permute-start | bytes 393224 | tf_op jit(solution)/shard_map/ppermute | solution.py:11
  89.0 14.2 %collective-permute-start.11 = (bf16[128,512]{1,0:T(8,128)(2,1)S(1)}, bf16[128,512]{1,0:T(8,128)(2,1)S(1)}, u32[]{:S(2)}, u32[]{:S(2)}) collective-permute-start(bf16[128,512]{1,0:T(8,128)(2,1)S(1)} %get-tuple-element.3), channel_id=1, source_target_pairs={{0,15},{1,0},{2,1},{3,2},{4,3},{5,4},{6,5},{7,6},{8,7},{9,8},{10,9... | collective-permute-start | bytes 393224 | tf_op jit(solution)/shard_map/ppermute | solution.py:11
